TPU v7x, 512 devices: a whole 4x8x8 slice. The times are simulated.
512 devices in a mesh: seq: 64 (over z, x, core), head: 8 (over y).
Axes of the slice: x: 4, y: 8, z: 8, core: 2. Of those that a mesh axis runs over, the one named last changes fastest.
Arguments:
- projected: float32 [65536, 2560], P(('seq', 'head')), may hold values from -6 to 6
- out_grads: float32 [65536, 2048], P(('seq', 'head')), may hold values from -6 to 6
- conv_weight: float32 [3, 2560], replicated, may hold values from -2.4 to 2.4
- doc_lengths: int32 [16], replicated, may hold values from 1 to 32768, 65536 in all
Outputs:
- grad_projected: float32 [65536, 2560], P(('seq', 'head'))
- grad_conv: float32 [3, 2560], replicated
Inputs may be any that keep to these rules, and one draw needn't show every extreme that they name: `doc_lengths`: the 16 documents fill the 65536 tokens end to end; the longest holds exactly half of 65536 tokens.
All inputs are finite; a program needn't handle non-finite values.
Results may differ from a plain program's by a relative error of at most 0.0003.
Values sent between devices are 32-bit elements; how exact they have to be, the bound alone decides.
No kernel may reach another device: no remote copies, remote signals or barrier semaphores. Data moves between devices by JAX's collectives and lax.ppermute only.
A program may use at most 128 MiB of HBM per device.

v0:
```python
import math

import jax
import jax.numpy as jnp
import numpy as np
from jax import lax
from jax.sharding import PartitionSpec as P

KEY_DIM = 16
HEAD_DIM = 128


HIGHEST = lax.Precision.HIGHEST


def carried_in(x, axis, combine, identity, reverse):
    length, here = (lax.axis_size(axis), lax.axis_index(axis))
    everything = jax.tree.map(lambda part: lax.all_gather(part, axis), x)
    start = jax.tree.map(
        lambda part, zero: jnp.broadcast_to(jnp.asarray(zero, part.dtype), part.shape), x, identity
    )

    def lap(k, before):
        at = length - 1 - k if reverse else k
        reached = at > here if reverse else at < here
        new = combine(before, jax.tree.map(lambda part: part[at], everything))
        return jax.tree.map(lambda a, b: jnp.where(reached, a, b), new, before)

    return lax.fori_loop(0, length, lap, start)


def passed_along(value, axis, steps):
    count = lax.axis_size(axis)
    initial, last = (max(0, -steps), min(count, count - steps))
    return lax.ppermute(value, axis, [(source, source + steps) for source in range(initial, last)])


def feature_map(columns):
    key_size = columns.shape[1]
    upper_i, upper_j = np.triu_indices(key_size)
    factors = np.where(upper_i == upper_j, 1.0 / math.sqrt(2.0), 1.0).astype(np.float32)
    products = columns[:, upper_i, :] * columns[:, upper_j, :] * jnp.asarray(factors)[None, :, None]
    constant = jnp.ones((columns.shape[0], 1, columns.shape[2]), jnp.float32)
    return jnp.concatenate([constant, columns, products], axis=1)


def doc_place(doc_lengths, anchor, amount):
    positions = anchor + jnp.arange(amount, dtype=jnp.int32)
    starts = jnp.cumsum(doc_lengths) - doc_lengths
    begins = jnp.max(jnp.where(starts[None, :] <= positions[:, None], starts[None, :], 0), axis=1)
    return (begins, positions - begins)


def conv_forward(signal, leading, weights, offsets):
    row_count = signal.shape[0]
    behind = jnp.concatenate([leading, signal], axis=0)
    back_one = behind[1 : row_count + 1] * (offsets[0:row_count] >= 1).astype(jnp.float32)[:, None]
    back_two = behind[0:row_count] * (offsets[0:row_count] >= 2).astype(jnp.float32)[:, None]
    return weights[0] * signal + weights[1] * back_one + weights[2] * back_two


def conv_backward(grad_rows, trailing, signal, leading, weights, offsets):
    row_count = grad_rows.shape[0]
    ahead_rows = jnp.concatenate([grad_rows, trailing], axis=0)
    ahead_one = (
        ahead_rows[1 : row_count + 1]
        * (offsets[1 : row_count + 1] >= 1).astype(jnp.float32)[:, None]
    )
    ahead_two = (
        ahead_rows[2 : row_count + 2]
        * (offsets[2 : row_count + 2] >= 2).astype(jnp.float32)[:, None]
    )
    grad_signal = weights[0] * grad_rows + weights[1] * ahead_one + weights[2] * ahead_two
    behind = jnp.concatenate([leading, signal], axis=0)
    own_one = (offsets[0:row_count] >= 1).astype(jnp.float32)[:, None]
    own_two = (offsets[0:row_count] >= 2).astype(jnp.float32)[:, None]
    grad_weights = jnp.stack(
        [
            jnp.sum(grad_rows * signal, axis=0),
            jnp.sum(grad_rows * behind[1 : row_count + 1] * own_one, axis=0),
            jnp.sum(grad_rows * behind[0:row_count] * own_two, axis=0),
        ],
        axis=0,
    )
    return (grad_signal, grad_weights)


def combine(earlier, following):
    carry_keep = 1.0 - following[2]
    return (
        following[0] + carry_keep[:, None, None] * earlier[0],
        following[1] + carry_keep[:, None] * earlier[1],
        jnp.maximum(earlier[2], following[2]),
    )


def attention_grads(mixed_rows, out_flat, begins, stretch_start):
    length = mixed_rows.shape[0]
    head_width = 2 * KEY_DIM + HEAD_DIM
    local_heads = mixed_rows.shape[1] // head_width
    block_len = min(128, length)
    blocks = length // block_len
    scale_key = KEY_DIM ** (-0.25)
    shaped = mixed_rows.reshape(length, local_heads, head_width)
    query_cols = jnp.transpose(shaped[:, :, :KEY_DIM], (1, 2, 0)) * scale_key
    key_cols = jnp.transpose(shaped[:, :, KEY_DIM : 2 * KEY_DIM], (1, 2, 0)) * scale_key
    values = shaped[:, :, 2 * KEY_DIM :]
    upstream = out_flat.reshape(length, local_heads, HEAD_DIM)
    query_feat, query_pull = jax.vjp(feature_map, query_cols)
    key_feat, key_pull = jax.vjp(feature_map, key_cols)
    feat_count = query_feat.shape[1]
    last_begin = begins[length - 1]
    has_start = (last_begin >= stretch_start).astype(jnp.float32).reshape(1)
    tail_mask = (begins == last_begin).astype(jnp.float32)
    tail_feat = key_feat * tail_mask[None, None, :]
    tail_state = jnp.einsum("hfl,lhe->hfe", tail_feat, values, precision=HIGHEST)
    tail_norm = jnp.sum(tail_feat, axis=2)
    identity = (jnp.zeros_like(tail_state), jnp.zeros_like(tail_norm), jnp.zeros((1,), jnp.float32))
    prefix = carried_in((tail_state, tail_norm, has_start), "seq", combine, identity, False)
    causal = jnp.arange(block_len)[:, None] >= jnp.arange(block_len)[None, :]
    indices = jnp.arange(blocks, dtype=jnp.int32)

    def forward_block(carried, block_index):
        carry_state, carry_norm = carried
        offset_rows = block_index * block_len
        block_start = stretch_start + offset_rows
        query_blk = lax.dynamic_slice_in_dim(query_feat, offset_rows, block_len, 2)
        key_blk = lax.dynamic_slice_in_dim(key_feat, offset_rows, block_len, 2)
        value_blk = lax.dynamic_slice_in_dim(values, offset_rows, block_len, 0)
        doc_blk = lax.dynamic_slice_in_dim(begins, offset_rows, block_len, 0)
        allowed = causal & (doc_blk[:, None] == doc_blk[None, :])
        scores = jnp.where(
            allowed[None], jnp.einsum("hft,hfs->hts", query_blk, key_blk, precision=HIGHEST), 0.0
        )
        from_carry = (doc_blk < block_start).astype(jnp.float32)
        numerator = jnp.einsum("hts,she->the", scores, value_blk, precision=HIGHEST) + from_carry[
            :, None, None
        ] * jnp.einsum("hft,hfe->the", query_blk, carry_state, precision=HIGHEST)
        denominator = jnp.sum(scores, axis=2) + from_carry[None, :] * jnp.einsum(
            "hft,hf->ht", query_blk, carry_norm, precision=HIGHEST
        )
        block_tail = (doc_blk == doc_blk[block_len - 1]).astype(jnp.float32)
        carry_keep = (doc_blk[block_len - 1] < block_start).astype(jnp.float32)
        tail_keys = key_blk * block_tail[None, None, :]
        next_state = (
            jnp.einsum("hfs,she->hfe", tail_keys, value_blk, precision=HIGHEST)
            + carry_keep * carry_state
        )
        next_norm = jnp.sum(tail_keys, axis=2) + carry_keep * carry_norm
        return ((next_state, next_norm), (numerator, denominator, carry_state, carry_norm, scores))

    forward_out = lax.scan(forward_block, (prefix[0], prefix[1]), indices)
    numerators, denominators, states, norms, kept_scores = forward_out[1]
    denom_rows = jnp.transpose(denominators, (0, 2, 1)).reshape(length, local_heads)
    attended = numerators.reshape(length, local_heads, HEAD_DIM) / denom_rows[:, :, None]
    grad_num = upstream / denom_rows[:, :, None]
    scalar_grad = -jnp.sum(upstream * attended, axis=2) / denom_rows
    lead_mask = (begins < stretch_start).astype(jnp.float32)
    lead_feat = query_feat * lead_mask[None, None, :]
    lead_state = jnp.einsum("hfl,lhe->hfe", lead_feat, grad_num, precision=HIGHEST)
    lead_norm = jnp.einsum("hfl,lh->hf", lead_feat, scalar_grad, precision=HIGHEST)
    suffix = carried_in((lead_state, lead_norm, has_start), "seq", combine, identity, True)

    def backward_block(carried, inputs):
        back_state, back_norm = carried
        block_index, carry_state, carry_norm, scores = inputs
        offset_rows = block_index * block_len
        block_start = stretch_start + offset_rows
        query_blk = lax.dynamic_slice_in_dim(query_feat, offset_rows, block_len, 2)
        key_blk = lax.dynamic_slice_in_dim(key_feat, offset_rows, block_len, 2)
        value_blk = lax.dynamic_slice_in_dim(values, offset_rows, block_len, 0)
        doc_blk = lax.dynamic_slice_in_dim(begins, offset_rows, block_len, 0)
        grad_blk = lax.dynamic_slice_in_dim(grad_num, offset_rows, block_len, 0)
        scalar_blk = lax.dynamic_slice_in_dim(scalar_grad, offset_rows, block_len, 0)
        scalar_cols = scalar_blk.T
        allowed = causal & (doc_blk[:, None] == doc_blk[None, :])
        dscores = jnp.where(
            allowed[None],
            jnp.einsum("the,she->hts", grad_blk, value_blk, precision=HIGHEST)
            + scalar_cols[:, :, None],
            0.0,
        )
        from_carry = (doc_blk < block_start).astype(jnp.float32)
        block_tail = (doc_blk == doc_blk[block_len - 1]).astype(jnp.float32)
        carry_keep = (doc_blk[block_len - 1] < block_start).astype(jnp.float32)
        grad_query = jnp.einsum("hts,hfs->hft", dscores, key_blk, precision=HIGHEST) + from_carry[
            None, None, :
        ] * (
            jnp.einsum("hfe,the->hft", carry_state, grad_blk, precision=HIGHEST)
            + carry_norm[:, :, None] * scalar_cols[:, None, :]
        )
        grad_key = jnp.einsum("hts,hft->hfs", dscores, query_blk, precision=HIGHEST) + block_tail[
            None, None, :
        ] * (
            jnp.einsum("hfe,she->hfs", back_state, value_blk, precision=HIGHEST)
            + back_norm[:, :, None]
        )
        grad_value = jnp.einsum("hts,the->she", scores, grad_blk, precision=HIGHEST) + block_tail[
            :, None, None
        ] * jnp.einsum("hfs,hfe->she", key_blk, back_state, precision=HIGHEST)
        lead_blk = query_blk * from_carry[None, None, :]
        next_state = (
            jnp.einsum("hft,the->hfe", lead_blk, grad_blk, precision=HIGHEST)
            + carry_keep * back_state
        )
        next_norm = (
            jnp.einsum("hft,th->hf", lead_blk, scalar_blk, precision=HIGHEST)
            + carry_keep * back_norm
        )
        return ((next_state, next_norm), (grad_query, grad_key, grad_value))

    swept_back = lax.scan(
        backward_block, (suffix[0], suffix[1]), (indices, states, norms, kept_scores), reverse=True
    )
    grad_qblocks, grad_kblocks, grad_vblocks = swept_back[1]
    query_grad = jnp.transpose(grad_qblocks, (1, 2, 0, 3)).reshape(local_heads, feat_count, length)
    key_grad = jnp.transpose(grad_kblocks, (1, 2, 0, 3)).reshape(local_heads, feat_count, length)
    value_grad = grad_vblocks.reshape(length, local_heads, HEAD_DIM)
    query_in = jnp.transpose(query_pull(query_grad)[0] * scale_key, (2, 0, 1))
    key_in = jnp.transpose(key_pull(key_grad)[0] * scale_key, (2, 0, 1))
    return jnp.concatenate([query_in, key_in, value_grad], axis=2).reshape(
        length, local_heads * head_width
    )


def on_device(projected, out_grads, conv_weight, doc_lengths):
    row_count = projected.shape[0]
    head_count = lax.axis_size("head")
    seq_index = lax.axis_index("seq")
    head_index = lax.axis_index("head")
    group_len = row_count * head_count
    token_base = (seq_index * head_count + head_index) * row_count
    stretch_start = seq_index * group_len
    token_begins, token_offsets = doc_place(doc_lengths, token_base, row_count + 2)
    leading = passed_along(projected[row_count - 2 :], ("seq", "head"), 1)
    outgoing = conv_forward(projected, leading, conv_weight, token_offsets)
    arrived, upstream = (
        lax.all_to_all(outgoing, "head", split_axis=1, concat_axis=0, tiled=True),
        lax.all_to_all(out_grads, "head", split_axis=1, concat_axis=0, tiled=True),
    )
    group_begins, group_offsets = doc_place(doc_lengths, stretch_start, group_len + 2)
    grad_mixed = attention_grads(arrived, upstream, group_begins[:group_len], stretch_start)
    returned = lax.all_to_all(grad_mixed, "head", split_axis=0, concat_axis=1, tiled=True)
    trailing = passed_along(returned[:2], ("seq", "head"), -1)
    grad_projected, weight_part = conv_backward(
        returned, trailing, projected, leading, conv_weight, token_offsets
    )
    grad_conv = lax.psum(weight_part, ("seq", "head"))
    return (grad_projected, grad_conv)


def solution(mesh):
    return jax.shard_map(
        on_device,
        mesh=mesh,
        in_specs=(P(("seq", "head"), None), P(("seq", "head"), None), P(), P()),
        out_specs=(P(("seq", "head"), None), P()),
        check_vma=False,
    )
```

profile of v0, /device:TPU:1, one launch (start us, length us, event | category | flops | bytes accessed | tf_op | source)
XLA Modules:
  0.0 1203.6 jit_solution(1783652886522364890)
XLA Ops:
  8.1 4.0 collective-permute-start
  17.7 3.1 multiply_add_fusion.1
  20.8 6.1 all-to-all-start
  28.4 33.2 %all-to-all-done = f32[128,8,320]{0,2,1:T(8,128)S(1)} async-done(((f32[128,8,320]{0,2,1:T(8,128)}), f32[128,8,320]{0,2,1:T(8,128)S(1)}, u32[]{:S(2)}, u32[]{:S(2)}) %all-to-all-start) | async-done | bytes 1310752 | tf_op jit(solution)/shard_map/all_to_all | solution.py:238
  64.6 3.1 gather_fusion.1
  73.7 3.1 fusion.91
  76.8 4.8 broadcast_multiply_fusion.1
  85.3 3.6 all-to-all-start.1
  91.7 131.3 %all-reduce = f32[64]{0:T(128)S(1)} all-reduce(f32[64]{0:T(128)S(1)} %dynamic-update-slice), channel_id=1, replica_groups=mesh['seq'=64,'head'=8] {'seq'}, use_global_device_ids=true, to_apply=%add | all-reduce | flops 64 | bytes 512
  232.5 51.4 %all-gather.4 = f32[64,2,153]{2,1,0:T(2,128)S(1)} all-gather(f32[1,2,153]{2,1,0:T(2,128)S(1)} %copy.127), channel_id=3, replica_groups=mesh['seq'=64,'head'=8] {'seq'}, dimensions={0}, use_global_device_ids=true | all-gather | bytes 79560 | tf_op jit(solution)/shard_map/all_gather | solution.py:18
  283.9 187.7 %while.82 = (s32[]{:T(128)}, f32[2,153,128]{2,1,0:T(8,128)S(1)}, f32[2,153]{1,0:T(2,128)S(1)}, s32[]{:T(128)}, f32[64,2,153,128]{3,2,1,0:T(8,128)}, /*index=5*/f...) while((s32[]{:T(128)}, f32[2,153,128]{2,1,0:T(8,128)S(1)}, ...), condition=%wide.region_5.6_spmd.clone, body=%wide.region_4.5_spmd.clone.sunk | while | flops 157901 | bytes 473831 | solution.py:29
  472.9 110.3 %while.80 = (s32[]{:T(128)}, f32[2,153,128]{2,1,0:T(8,128)S(1)}, f32[2,153]{1,0:T(2,128)S(1)}, f32[8,128,2,128]{1,0,3,2:T(8,128)}, f32[8,2,128]{2,1,0:T(2,128)S(...) while((s32[]{:T(128)}, f32[2,153,128]{2,1,0:T(8,128)S(1)}, ...), condition=%wide.region_9.10_spmd.clone, body=%wide.region_6.9_spmd.clone.sunk | while | flops 231664960 | bytes 3280461 | solution.py:152
  476.9 4.8 dynamic_update_slice.74
  490.7 4.8 dynamic_update_slice.74
  504.5 4.8 dynamic_update_slice.74
  518.3 4.8 dynamic_update_slice.74
  532.1 4.8 dynamic_update_slice.74
  545.9 4.8 dynamic_update_slice.74
  559.7 4.8 dynamic_update_slice.74
  573.4 4.8 dynamic_update_slice.74
  593.5 49.5 %all-gather.5 = f32[64,2,153]{2,1,0:T(2,128)S(1)} all-gather(f32[1,2,153]{2,1,0:T(2,128)S(1)} %bitcast.282), channel_id=5, replica_groups=mesh['seq'=64,'head'=8] {'seq'}, dimensions={0}, use_global_device_ids=true | all-gather | bytes 79560 | tf_op jit(solution)/shard_map/all_gather | solution.py:18
  643.0 36.5 %all-gather.11.cloned.1.call-done = f32[128,153,128]{2,1,0:T(8,128)} async-done(((f32[2,153,128]{2,1,0:T(8,128)}), f32[128,153,128]{2,1,0:T(8,128)}) %all-gather.11.cloned.1.call-update) | async-done | bytes 10027024 | tf_op jit(solution)/shard_map/all_gather | solution.py:18
  679.5 195.2 %while.83 = (s32[]{:T(128)}, f32[2,153,128]{2,1,0:T(8,128)S(1)}, f32[2,153]{1,0:T(2,128)S(1)}, s32[]{:T(128)}, f32[64,2,153,128]{3,2,1,0:T(8,128)}, /*index=5*/f...) while((s32[]{:T(128)}, f32[2,153,128]{2,1,0:T(8,128)S(1)}, ...), condition=%wide.region_12.13_spmd.clone, body=%wide.region_11.12_spmd.clone.sunk | while | flops 157905 | bytes 473893 | solution.py:29
  878.2 112.1 %while.81 = (s32[]{:T(128)}, f32[2,153,128]{2,1,0:T(8,128)S(1)}, f32[2,153]{1,0:T(2,128)S(1)}, f32[8,2,153,128]{3,2,1,0:T(8,128)}, f32[8,2,153,128]{3,2,1,0:T(8,...) while((s32[]{:T(128)}, f32[2,153,128]{2,1,0:T(8,128)S(1)}, ...), condition=%wide.region_14.15_spmd.clone, body=%wide.region_13.14_spmd.clone.sunk | while | flops 462717824 | bytes 4866477 | solution.py:212
  998.9 5.9 fusion.90
  1004.9 14.0 %scatter_fusion = f32[2,16,1024]{2,0,1:T(2,128)S(1)} fusion(f32[2,16,1024]{2,0,1:T(2,128)S(1)} %split.16, s32[136]{0:T(256)S(1)} %copy-done.23, f32[136,2,1024]{2,1,0:T(2,128)} %get-tuple-element.1103), kind=kCustom, calls=%fused_computation.4 | custom fusion | flops 278528 | bytes 3342880 | tf_op jit(solution)/shard_map/transpose(jvp())/scatter-add | solution.py:42
  1018.9 7.6 scatter_fusion.1
  1027.7 7.6 scatter_fusion.3
  1035.3 7.6 scatter_fusion.2
  1048.3 40.7 %all_to_all.51 = f32[8,128,320]{1,2,0:T(8,128)S(1)} all-to-all(f32[8,128,320]{1,2,0:T(8,128)S(1)} %copy.143), channel_id=1, replica_groups=mesh['seq'=64,'head'=8] {'head'}, dimensions={0} | all-to-all | bytes 2621440 | tf_op jit(solution)/shard_map/all_to_all | solution.py:243
  1093.7 95.5 %psum.7 = f32[3,2560]{1,0:T(4,128)} all-reduce(f32[3,2560]{1,0:T(4,128)S(1)} %pad_maximum_fusion.5), channel_id=1, replica_groups=mesh['seq'=64,'head'=8] {'seq','head'}, use_global_device_ids=true, to_apply=%region_22.23 | all-reduce | flops 7680 | bytes 61440 | tf_op jit(solution)/shard_map/psum | solution.py:248
  1190.7 4.4 fusion.77
  (830 shorter events, 611.8 us)
Async XLA Ops:
  8.1 9.1 collective-permute-start
  14.4 3.2 copy-start.25
  14.4 3.2 copy-start.27
  15.4 2.2 copy-start.16
  17.2 3.6 copy-start.3
  17.6 3.1 copy-start.5
  20.8 6.9 copy-start.24
  20.8 6.9 copy-start.23
  20.8 40.9 %all-to-all-start = ((f32[128,8,320]{0,2,1:T(8,128)}), f32[128,8,320]{0,2,1:T(8,128)S(1)}, u32[]{:S(2)}, u32[]{:S(2)}) async-start(f32[128,8,320]{0,2,1:T(8,128)} %bitcast.265), calls=%async_computation | async-start | bytes 2621440 | tf_op jit(solution)/shard_map/all_to_all | solution.py:238
  26.9 257.1 %all-gather.9.cloned.1.call-start = ((), (), s32[]{:S(2)}) async-start(), calls=%async_computation.3 | async-start | bytes 10649600 | tf_op jit(solution)/shard_map/all_gather | solution.py:18
  27.0 62.6 %copy-start.22 = (s32[1026]{0:T(1024)}, s32[1026]{0:T(1024)S(1)}, u32[]{:S(2)}) copy-start(s32[1026]{0:T(1024)S(1)} %select_reduce_fusion) | copy-start | bytes 12316
  64.6 9.1 copy-start.7
  70.7 3.0 copy-start.29
  81.6 2.3 copy-start.15
  85.3 137.7 %all-to-all-start.1 = ((f32[128,8,256]{0,2,1:T(8,128)}), f32[128,8,256]{0,2,1:T(8,128)S(1)}, u32[]{:S(2)}, u32[]{:S(2)}) async-start(f32[128,8,256]{0,2,1:T(8,128)} %bitcast.273), calls=%async_computation.1 | async-start | bytes 2097152 | tf_op jit(solution)/shard_map/all_to_all | solution.py:239
  88.8 590.7 %all-gather.11.cloned.1.call-start = ((), (), s32[]{:S(2)}) async-start(), calls=%async_computation.4 | async-start | bytes 10649600 | tf_op jit(solution)/shard_map/all_gather | solution.py:18
  585.5 2.9 copy-start.2
  995.9 3.1 copy-start.8
  997.8 7.0 copy-start.1
  1004.9 14.0 %copy-start.14 = (f32[136,2,1024]{2,1,0:T(2,128)S(1)}, f32[136,2,1024]{2,1,0:T(2,128)}, u32[]{:S(2)}) copy-start(f32[136,2,1024]{2,1,0:T(2,128)} %get-tuple-element.1102) | copy-start | bytes 3342340
  1027.7 7.6 slice-start
  1027.7 7.6 copy-start.12
  1048.0 41.0 %copy-start.26 = (f32[128]{0:T(128)S(1)}, f32[128]{0:T(128)}, u32[]{:S(2)}) copy-start(f32[128]{0:T(128)} %copy-done.25) | copy-start | bytes 1540
  1048.1 41.0 %copy-start.28 = (f32[128]{0:T(128)S(1)}, f32[128]{0:T(128)}, u32[]{:S(2)}) copy-start(f32[128]{0:T(128)} %copy-done.27) | copy-start | bytes 1540
  1048.3 40.7 %copy-start.4 = (f32[128,2560]{0,1:T(8,128)S(1)}, f32[128,2560]{0,1:T(8,128)}, u32[]{:S(2)}) copy-start(f32[128,2560]{0,1:T(8,128)} %copy-done.3) | copy-start | bytes 3932164
  1048.3 40.7 %copy-start.6 = (f32[2,2560]{0,1:T(8,128)S(1)}, f32[2,2560]{0,1:T(8,128)}, u32[]{:S(2)}) copy-start(f32[2,2560]{0,1:T(8,128)} %copy-done.5) | copy-start | bytes 61444
  1091.3 99.4 %copy-start.17 = (f32[2560]{0:T(1024)S(1)}, f32[2560]{0:T(1024)}, u32[]{:S(2)}) copy-start(f32[2560]{0:T(1024)} %copy-done.16) | copy-start | bytes 30724
  1091.3 99.4 %copy-start.19 = (f32[2560]{0:T(1024)S(1)}, f32[2560]{0:T(1024)}, u32[]{:S(2)}) copy-start(f32[2560]{0:T(1024)} %copy-done.18) | copy-start | bytes 30724
  1091.3 99.4 %copy-start.21 = (f32[2560]{0:T(1024)S(1)}, f32[2560]{0:T(1024)}, u32[]{:S(2)}) copy-start(f32[2560]{0:T(1024)} %copy-done.20) | copy-start | bytes 30724
  1091.3 99.4 %copy-start.30 = (f32[128]{0:T(128)S(1)}, f32[128]{0:T(128)}, u32[]{:S(2)}) copy-start(f32[128]{0:T(128)} %get-tuple-element.1110) | copy-start | bytes 1540
  1091.3 99.4 %copy-start.31 = (f32[128]{0:T(128)S(1)}, f32[128]{0:T(128)}, u32[]{:S(2)}) copy-start(f32[128]{0:T(128)} %get-tuple-element.1112) | copy-start | bytes 1540
  1091.7 97.5 %collective-permute-start.1 = (f32[2,2560]{1,0:T(2,128)S(1)}, f32[2,2560]{1,0:T(2,128)S(1)}, u32[]{:S(2)}, u32[]{:S(2)}) collective-permute-start(f32[2,2560]{1,0:T(2,128)S(1)} %copy.144), channel_id=1, source_target_pairs={{1,0},{2,1},{3,2},{4,3},{5,4},{6,5},{7,6},{8,7},{9,8},{10,9},{11,1... | collective-permute-start | bytes 61448 | tf_op jit(solution)/shard_map/ppermute | solution.py:35
  (8 other events, 12.7 us)
Sparse Core Ops, SparseCore 0:
  84.0 91.8 all-gather.8
  590.8 88.6 all-gather.10
where the time goes:
time: 1220 us; the launch traced here: 1200 us
  other arithmetic  462 us (38%)
  blocking collectives  368 us (30%)
  local copies, waits for them, and re-layouts  129 us (11%)
  matrix products  118 us (10%)
  waiting for transfers between devices  69.8 us (6%)
  loops' own time  25.3 us (2%)
  starting transfers between devices  15.7 us (1%)
  between operations  15.7 us (1%)
    select_n x256, other arithmetic, lap(): return jax.tree.map(lambda a, b: jnp.where(reached, a, b), new, before)  301 us
    unnamed x1, blocking collectives  131 us
    all_gather x2, blocking collectives, carried_in(): everything = jax.tree.map(lambda part: lax.all_gather(part, axis), x)  101 us
    psum x1, blocking collectives, on_device(): grad_conv = lax.psum(weight_part, ('seq', 'head'))  95.5 us
    sub x128, other arithmetic, combine(): carry_keep = 1.0 - following[2]  78.9 us
    dynamic_update_slice x48, local copies, waits for them, and re-layouts, attention_grads(): forward_out = lax.scan(forward_block, (prefix[0], prefix[1]), indices)  55 us
    all_to_all x1, blocking collectives, on_device(): lax.all_to_all(grad_mixed, 'head', split_axis=0, concat_axis=1, tiled=True)  40.7 us
    all_gather x2, waiting for transfers between devices, carried_in(): everything = jax.tree.map(lambda part: lax.all_gather(part, axis), x)  36.5 us
  transfers between devices with their start and end apart: 6, of which 2 were waited for; matrix products, arithmetic and copies ran while one was open for 2% of the time, Pallas kernels for 0%

commit v1 on v0

--- a/solution.py
+++ b/solution.py
@@ -13,20 +13,30 @@
 HIGHEST = lax.Precision.HIGHEST
 
 
-def carried_in(x, axis, combine, identity, reverse):
-    length, here = (lax.axis_size(axis), lax.axis_index(axis))
-    everything = jax.tree.map(lambda part: lax.all_gather(part, axis), x)
-    start = jax.tree.map(
-        lambda part, zero: jnp.broadcast_to(jnp.asarray(zero, part.dtype), part.shape), x, identity
-    )
-
-    def lap(k, before):
-        at = length - 1 - k if reverse else k
-        reached = at > here if reverse else at < here
-        new = combine(before, jax.tree.map(lambda part: part[at], everything))
-        return jax.tree.map(lambda a, b: jnp.where(reached, a, b), new, before)
-
-    return lax.fori_loop(0, length, lap, start)
+def segment_sum(gathered, flags, here, reverse):
+    count = gathered.shape[0]
+    index = jnp.arange(count, dtype=jnp.int32)
+    started = flags > 0.5
+    if reverse:
+        bound = jnp.min(jnp.where((index > here) & started, index, count - 1))
+        take = (index > here) & (index <= bound)
+    else:
+        bound = jnp.max(jnp.where((index < here) & started, index, 0))
+        take = (index >= bound) & (index < here)
+    return jnp.sum(jnp.where(take[:, None], gathered, 0.0), axis=0)
+
+
+def carried_in(state, norm, extra, flags, axis, reverse):
+    here = lax.axis_index(axis)
+    size = state.size
+    packed = jnp.concatenate([state.reshape(-1), norm.reshape(-1), extra])
+    width = 128
+    padded = jnp.pad(packed, (0, -packed.shape[0] % width)).reshape(-1, width)
+    gathered = lax.all_gather(padded, axis).reshape(lax.axis_size(axis), -1)
+    if flags is None:
+        flags = gathered[:, packed.shape[0] - 1]
+    total = segment_sum(gathered[:, : size + norm.size], flags, here, reverse)
+    return (total[:size].reshape(state.shape), total[size:].reshape(norm.shape), flags)
 
 
 def passed_along(value, axis, steps):
@@ -83,15 +93,6 @@
         axis=0,
     )
     return (grad_signal, grad_weights)
-
-
-def combine(earlier, following):
-    carry_keep = 1.0 - following[2]
-    return (
-        following[0] + carry_keep[:, None, None] * earlier[0],
-        following[1] + carry_keep[:, None] * earlier[1],
-        jnp.maximum(earlier[2], following[2]),
-    )
 
 
 def attention_grads(mixed_rows, out_flat, begins, stretch_start):
@@ -115,8 +116,8 @@
     tail_feat = key_feat * tail_mask[None, None, :]
     tail_state = jnp.einsum("hfl,lhe->hfe", tail_feat, values, precision=HIGHEST)
     tail_norm = jnp.sum(tail_feat, axis=2)
-    identity = (jnp.zeros_like(tail_state), jnp.zeros_like(tail_norm), jnp.zeros((1,), jnp.float32))
-    prefix = carried_in((tail_state, tail_norm, has_start), "seq", combine, identity, False)
+    prefix = carried_in(tail_state, tail_norm, has_start, None, "seq", False)
+    flags = prefix[2]
     causal = jnp.arange(block_len)[:, None] >= jnp.arange(block_len)[None, :]
     indices = jnp.arange(blocks, dtype=jnp.int32)
 
@@ -159,7 +160,7 @@
     lead_feat = query_feat * lead_mask[None, None, :]
     lead_state = jnp.einsum("hfl,lhe->hfe", lead_feat, grad_num, precision=HIGHEST)
     lead_norm = jnp.einsum("hfl,lh->hf", lead_feat, scalar_grad, precision=HIGHEST)
-    suffix = carried_in((lead_state, lead_norm, has_start), "seq", combine, identity, True)
+    suffix = carried_in(lead_state, lead_norm, jnp.zeros((0,), jnp.float32), flags, "seq", True)
 
     def backward_block(carried, inputs):
         back_state, back_norm = carried

time: 1220 us -> 743 us (0.61)
  other arithmetic: 462 us -> 85.8 us
  blocking collectives: 368 us -> 137 us
  waiting for transfers between devices: 69.8 us -> 198 us
  local copies, waits for them, and re-layouts: 129 us -> 146 us
    select_n x256 -> x0, other arithmetic: 301 us -> none  [lap(): return jax.tree.map(lambda a, b: jnp.where(reached, a, b), new, before)]
    unnamed x1 -> x0, blocking collectives: 131 us -> none
    all_gather x2 -> x0, blocking collectives: 101 us -> none  [carried_in(): everything = jax.tree.map(lambda part: lax.all_gather(part, axis), x)]
    all_gather x2, waiting for transfers between devices: 36.5 us -> 136 us  [carried_in(): gathered = lax.all_gather(padded, axis).reshape(lax.axis_size(axis), -1)]
    sub x128 -> x0, other arithmetic: 78.9 us -> none  [combine(): carry_keep = 1.0 - following[2]]
    all_to_all x1, waiting for transfers between devices: 0.01 us -> 28.9 us  [on_device(): lax.all_to_all(out_grads, 'head', split_axis=1, concat_axis=0, tiled=True)]
  transfers between devices with their start and end apart: 6 -> 6, of which waited for: 2 -> 4; matrix products, arithmetic and copies ran while one was open for 2% -> 2% of each run, Pallas kernels for 0% -> 0%
where the time goes in v1:
time: 743 us; the launch traced here: 737 us
  waiting for transfers between devices  198 us (27%)
  local copies, waits for them, and re-layouts  146 us (20%)
  blocking collectives  137 us (18%)
  matrix products  117 us (16%)
  other arithmetic  85.8 us (12%)
  loops' own time  22.4 us (3%)
  starting transfers between devices  15.8 us (2%)
  between operations  15.5 us (2%)
    all_gather x2, waiting for transfers between devices, carried_in(): gathered = lax.all_gather(padded, axis).reshape(lax.axis_size(axis), -1)  136 us
    psum x1, blocking collectives, on_device(): grad_conv = lax.psum(weight_part, ('seq', 'head'))  95.7 us
    dynamic_update_slice x48, local copies, waits for them, and re-layouts, attention_grads(): forward_out = lax.scan(forward_block, (prefix[0], prefix[1]), indices)  55 us
    all_to_all x1, blocking collectives, on_device(): lax.all_to_all(grad_mixed, 'head', split_axis=0, concat_axis=1, tiled=True)  41 us
    all_to_all x1, waiting for transfers between devices, on_device(): lax.all_to_all(outgoing, 'head', split_axis=1, concat_axis=0, tiled=True)  32.9 us
    all_to_all x1, waiting for transfers between devices, on_device(): lax.all_to_all(out_grads, 'head', split_axis=1, concat_axis=0, tiled=True)  28.9 us
    unnamed x48, local copies, waits for them, and re-layouts  23.9 us
    scatter-add x2, other arithmetic, feature_map(): columns[:, upper_j, :]  21.3 us
  transfers between devices with their start and end apart: 6, of which 4 were waited for; matrix products, arithmetic and copies ran while one was open for 2% of the time, Pallas kernels for 0%

profile of v1, /device:TPU:1, one launch (start us, length us, event | category | flops | bytes accessed | tf_op | source)
XLA Modules:
  0.0 737.0 jit_solution(17403635177316418319)
XLA Ops:
  8.1 4.0 collective-permute-start
  17.0 3.1 multiply_add_fusion.1
  20.1 6.1 all-to-all-start
  28.1 32.9 %all-to-all-done = f32[128,8,320]{0,2,1:T(8,128)S(1)} async-done(((f32[128,8,320]{0,2,1:T(8,128)}), f32[128,8,320]{0,2,1:T(8,128)S(1)}, u32[]{:S(2)}, u32[]{:S(2)}) %all-to-all-start) | async-done | bytes 1310752 | tf_op jit(solution)/shard_map/all_to_all | solution.py:239
  65.0 3.0 gather_fusion
  68.1 3.1 gather_fusion.1
  77.2 3.4 fusion.89
  80.6 4.3 fusion.98
  88.8 3.6 all-to-all-start.1
  92.7 28.9 %all-to-all-done.1 = f32[128,8,256]{0,2,1:T(8,128)S(1)} async-done(((f32[128,8,256]{0,2,1:T(8,128)}), f32[128,8,256]{0,2,1:T(8,128)S(1)}, u32[]{:S(2)}, u32[]{:S(2)}) %all-to-all-start.1) | async-done | bytes 1048608 | tf_op jit(solution)/shard_map/all_to_all | solution.py:240
  131.0 48.2 %all-gather.3.cloned.1.call-done = f32[64,309,128]{2,1,0:T(8,128)} async-done(((f32[1,309,128]{2,1,0:T(8,128)}), f32[64,309,128]{2,1,0:T(8,128)}) %all-gather.3.cloned.1.call-update) | async-done | bytes 10125328 | tf_op jit(solution)/shard_map/all_gather | solution.py:35
  179.2 5.7 copy.305
  188.8 110.3 %while.46 = (s32[]{:T(128)}, f32[2,153,128]{2,1,0:T(8,128)S(1)}, f32[2,153]{1,0:T(2,128)S(1)}, f32[8,128,2,128]{1,0,3,2:T(8,128)}, f32[8,2,128]{2,1,0:T(2,128)S(...) while((s32[]{:T(128)}, f32[2,153,128]{2,1,0:T(8,128)S(1)}, ...), condition=%wide.region_10.11_spmd.clone, body=%wide.region_7.10_spmd.clone.sunk | while | flops 231664960 | bytes 3280461 | solution.py:153
  192.8 4.8 dynamic_update_slice.74
  206.6 4.8 dynamic_update_slice.74
  220.4 4.8 dynamic_update_slice.74
  234.2 4.8 dynamic_update_slice.74
  248.0 4.8 dynamic_update_slice.74
  261.8 4.8 dynamic_update_slice.74
  275.6 4.8 dynamic_update_slice.74
  289.3 4.8 dynamic_update_slice.74
  310.3 88.0 %all-gather.5.cloned.1.call-done = f32[64,309,128]{2,1,0:T(8,128)} async-done(((f32[1,309,128]{2,1,0:T(8,128)}), f32[64,309,128]{2,1,0:T(8,128)}) %all-gather.5.cloned.1.call-update) | async-done | bytes 10125328 | tf_op jit(solution)/shard_map/all_gather | solution.py:35
  398.3 5.7 copy.304
  408.5 112.2 %while.47 = (s32[]{:T(128)}, f32[2,153,128]{2,1,0:T(8,128)S(1)}, f32[2,153]{1,0:T(2,128)S(1)}, f32[8,2,153,128]{3,2,1,0:T(8,128)}, f32[8,2,153,128]{3,2,1,0:T(8,...) while((s32[]{:T(128)}, f32[2,153,128]{2,1,0:T(8,128)S(1)}, ...), condition=%wide.region_14.15_spmd.clone, body=%wide.region_13.14_spmd.clone.sunk | while | flops 462717824 | bytes 4866477 | solution.py:213
  529.4 6.0 fusion.85
  535.3 14.0 %scatter_fusion = f32[2,16,1024]{2,0,1:T(2,128)S(1)} fusion(f32[2,16,1024]{2,0,1:T(2,128)S(1)} %split.16, s32[136]{0:T(256)S(1)} %copy-done.16, f32[136,2,1024]{2,1,0:T(2,128)} %get-tuple-element.822), kind=kCustom, calls=%fused_computation.4 | custom fusion | flops 278528 | bytes 3342880 | tf_op jit(solution)/shard_map/transpose(jvp())/scatter-add | solution.py:52
  549.4 7.6 %scatter_fusion.1 = f32[2,16,1024]{2,0,1:T(2,128)S(1)} fusion(f32[2,16,1024]{2,0,1:T(2,128)S(1)} %broadcast.144.clone.1, s32[136]{0:T(256)S(1)} %copy-done.17, f32[136,2,1024]{2,1,0:T(2,128)S(1)} %copy-done.13), kind=kCustom, calls=%fused_computation.5 | custom fusion | flops 278528 | bytes 3342880 | tf_op jit(solution)/shard_map/transpose(jvp())/scatter-add | solution.py:52
  558.4 7.6 %scatter_fusion.3 = f32[2,16,1024]{2,0,1:T(2,128)S(1)} fusion(f32[2,16,1024]{2,0,1:T(2,128)S(1)} %broadcast.144.clone, s32[136]{0:T(256)S(1)} %copy-done.17, f32[136,2,1024]{2,1,0:T(2,128)S(1)} %copy-done.12), kind=kCustom, calls=%fused_computation.7 | custom fusion | flops 278528 | bytes 3342880 | tf_op jit(solution)/shard_map/transpose(jvp())/scatter-add | solution.py:52
  566.0 7.3 scatter_fusion.2
  581.3 41.0 %all_to_all.51 = f32[8,128,320]{1,2,0:T(8,128)S(1)} all-to-all(f32[8,128,320]{1,2,0:T(8,128)S(1)} %copy.248), channel_id=1, replica_groups=mesh['seq'=64,'head'=8] {'head'}, dimensions={0} | all-to-all | bytes 2621440 | tf_op jit(solution)/shard_map/all_to_all | solution.py:244
  626.8 95.7 %psum.7 = f32[3,2560]{1,0:T(4,128)} all-reduce(f32[3,2560]{1,0:T(4,128)S(1)} %pad_maximum_fusion.5), channel_id=1, replica_groups=mesh['seq'=64,'head'=8] {'seq','head'}, use_global_device_ids=true, to_apply=%region_22.23 | all-reduce | flops 7680 | bytes 61440 | tf_op jit(solution)/shard_map/psum | solution.py:249
  724.1 4.3 fusion.75
  (429 shorter events, 237.6 us)
Async XLA Ops:
  8.1 8.5 %collective-permute-start = (f32[2,2560]{1,0:T(2,128)S(1)}, f32[2,2560]{1,0:T(2,128)S(1)}, u32[]{:S(2)}, u32[]{:S(2)}) collective-permute-start(f32[2,2560]{1,0:T(2,128)S(1)} %slice.116), channel_id=1, source_target_pairs={{0,1},{1,2},{2,3},{3,4},{4,5},{5,6},{6,7},{7,8},{8,9},{9,10},{10,1... | collective-permute-start | bytes 61448 | tf_op jit(solution)/shard_map/ppermute | solution.py:45
  16.6 3.5 copy-start.3
  17.0 3.1 copy-start.5
  20.1 7.4 %copy-start.17 = (s32[136]{0:T(256)S(1)}, s32[136]{0:T(256)}, u32[]{:S(2)}) copy-start(s32[136]{0:T(256)} %constant.158) | copy-start | bytes 1636
  20.1 7.4 %copy-start.16 = (s32[136]{0:T(256)S(1)}, s32[136]{0:T(256)}, u32[]{:S(2)}) copy-start(s32[136]{0:T(256)} %constant.159) | copy-start | bytes 1636
  20.1 40.9 %all-to-all-start = ((f32[128,8,320]{0,2,1:T(8,128)}), f32[128,8,320]{0,2,1:T(8,128)S(1)}, u32[]{:S(2)}, u32[]{:S(2)}) async-start(f32[128,8,320]{0,2,1:T(8,128)} %bitcast.248), calls=%async_computation | async-start | bytes 2621440 | tf_op jit(solution)/shard_map/all_to_all | solution.py:239
  26.2 153.0 %all-gather.3.cloned.1.call-start = ((), (), s32[]{:S(2)}) async-start(), calls=%async_computation.3 | async-start | bytes 10383360 | tf_op jit(solution)/shard_map/all_gather | solution.py:35
  26.3 66.3 %copy-start.15 = (s32[1026]{0:T(1024)}, s32[1026]{0:T(1024)S(1)}, u32[]{:S(2)}) copy-start(s32[1026]{0:T(1024)S(1)} %select_reduce_fusion) | copy-start | bytes 12316
  74.2 3.0 copy-start.18
  84.9 2.6 copy-start.14
  88.8 32.7 %all-to-all-start.1 = ((f32[128,8,256]{0,2,1:T(8,128)}), f32[128,8,256]{0,2,1:T(8,128)S(1)}, u32[]{:S(2)}, u32[]{:S(2)}) async-start(f32[128,8,256]{0,2,1:T(8,128)} %bitcast.256), calls=%async_computation.1 | async-start | bytes 2097152 | tf_op jit(solution)/shard_map/all_to_all | solution.py:240
  92.4 305.8 %all-gather.5.cloned.1.call-start = ((), (), s32[]{:S(2)}) async-start(), calls=%async_computation.4 | async-start | bytes 10383360 | tf_op jit(solution)/shard_map/all_gather | solution.py:35
  125.5 1.7 copy-start.10
  126.6 1.4 copy-start.9
  187.4 1.3 slice-start.1
  301.4 2.9 copy-start.2
  303.3 1.0 copy-start
  522.8 1.7 copy-start.8
  526.3 3.1 copy-start.7
  528.3 7.1 copy-start.1
  535.3 14.0 %copy-start.13 = (f32[136,2,1024]{2,1,0:T(2,128)S(1)}, f32[136,2,1024]{2,1,0:T(2,128)}, u32[]{:S(2)}) copy-start(f32[136,2,1024]{2,1,0:T(2,128)} %get-tuple-element.821) | copy-start | bytes 3342340
  557.0 1.4 copy-start.12
  558.4 7.6 %slice-start = ((f32[2,153,1024]{2,0,1:T(2,128)}), f32[2,16,1024]{2,0,1:T(2,128)S(1)}, s32[]{:S(2)}) async-start(f32[2,153,1024]{2,0,1:T(2,128)} %copy-done.1), calls=%async_computation.5 | async-start | bytes 262144 | tf_op jit(solution)/shard_map/transpose(jvp())/split | solution.py:54
  558.4 7.6 %copy-start.11 = (f32[136,2,1024]{2,1,0:T(2,128)S(1)}, f32[136,2,1024]{2,1,0:T(2,128)}, u32[]{:S(2)}) copy-start(f32[136,2,1024]{2,1,0:T(2,128)} %get-tuple-element.833) | copy-start | bytes 3342340
  581.3 41.0 %copy-start.4 = (f32[128,2560]{0,1:T(8,128)S(1)}, f32[128,2560]{0,1:T(8,128)}, u32[]{:S(2)}) copy-start(f32[128,2560]{0,1:T(8,128)} %copy-done.3) | copy-start | bytes 3932164
  581.3 41.0 %copy-start.6 = (f32[2,2560]{0,1:T(8,128)S(1)}, f32[2,2560]{0,1:T(8,128)}, u32[]{:S(2)}) copy-start(f32[2,2560]{0,1:T(8,128)} %copy-done.5) | copy-start | bytes 61444
  624.9 97.7 %collective-permute-start.1 = (f32[2,2560]{1,0:T(2,128)S(1)}, f32[2,2560]{1,0:T(2,128)S(1)}, u32[]{:S(2)}, u32[]{:S(2)}) collective-permute-start(f32[2,2560]{1,0:T(2,128)S(1)} %copy.249), channel_id=1, source_target_pairs={{1,0},{2,1},{3,2},{4,3},{5,4},{6,5},{7,6},{8,7},{9,8},{10,9},{11,1... | collective-permute-start | bytes 61448 | tf_op jit(solution)/shard_map/ppermute | solution.py:45
Sparse Core Ops, SparseCore 0:
  87.6 91.5 all-gather.2
  309.7 88.5 all-gather.4

commit v2 on v1

--- a/solution.py
+++ b/solution.py
@@ -119,39 +119,40 @@
     prefix = carried_in(tail_state, tail_norm, has_start, None, "seq", False)
     flags = prefix[2]
     causal = jnp.arange(block_len)[:, None] >= jnp.arange(block_len)[None, :]
-    indices = jnp.arange(blocks, dtype=jnp.int32)
-
-    def forward_block(carried, block_index):
-        carry_state, carry_norm = carried
-        offset_rows = block_index * block_len
-        block_start = stretch_start + offset_rows
-        query_blk = lax.dynamic_slice_in_dim(query_feat, offset_rows, block_len, 2)
-        key_blk = lax.dynamic_slice_in_dim(key_feat, offset_rows, block_len, 2)
-        value_blk = lax.dynamic_slice_in_dim(values, offset_rows, block_len, 0)
-        doc_blk = lax.dynamic_slice_in_dim(begins, offset_rows, block_len, 0)
-        allowed = causal & (doc_blk[:, None] == doc_blk[None, :])
-        scores = jnp.where(
-            allowed[None], jnp.einsum("hft,hfs->hts", query_blk, key_blk, precision=HIGHEST), 0.0
-        )
-        from_carry = (doc_blk < block_start).astype(jnp.float32)
-        numerator = jnp.einsum("hts,she->the", scores, value_blk, precision=HIGHEST) + from_carry[
-            :, None, None
-        ] * jnp.einsum("hft,hfe->the", query_blk, carry_state, precision=HIGHEST)
-        denominator = jnp.sum(scores, axis=2) + from_carry[None, :] * jnp.einsum(
-            "hft,hf->ht", query_blk, carry_norm, precision=HIGHEST
-        )
-        block_tail = (doc_blk == doc_blk[block_len - 1]).astype(jnp.float32)
-        carry_keep = (doc_blk[block_len - 1] < block_start).astype(jnp.float32)
-        tail_keys = key_blk * block_tail[None, None, :]
-        next_state = (
-            jnp.einsum("hfs,she->hfe", tail_keys, value_blk, precision=HIGHEST)
-            + carry_keep * carry_state
-        )
-        next_norm = jnp.sum(tail_keys, axis=2) + carry_keep * carry_norm
-        return ((next_state, next_norm), (numerator, denominator, carry_state, carry_norm, scores))
-
-    forward_out = lax.scan(forward_block, (prefix[0], prefix[1]), indices)
-    numerators, denominators, states, norms, kept_scores = forward_out[1]
+    query_blk = jnp.transpose(query_feat.reshape(local_heads, feat_count, blocks, block_len), (2, 0, 1, 3))
+    key_blk = jnp.transpose(key_feat.reshape(local_heads, feat_count, blocks, block_len), (2, 0, 1, 3))
+    value_blk = values.reshape(blocks, block_len, local_heads, HEAD_DIM)
+    doc_blk = begins.reshape(blocks, block_len)
+    block_start = stretch_start + jnp.arange(blocks, dtype=jnp.int32) * block_len
+    allowed = causal[None] & (doc_blk[:, :, None] == doc_blk[:, None, :])
+    from_carry = (doc_blk < block_start[:, None]).astype(jnp.float32)
+    block_tail = (doc_blk == doc_blk[:, block_len - 1 :]).astype(jnp.float32)
+    breaks = (doc_blk[:, block_len - 1] >= block_start).astype(jnp.int32)
+    upto = jnp.cumsum(breaks)
+    before = upto - breaks
+    order = jnp.arange(blocks)
+    ahead_w = ((order[None, :] < order[:, None]) & (before[:, None] == upto[None, :])).astype(jnp.float32)
+    ahead_p = (before == 0).astype(jnp.float32)
+    behind_w = ((order[None, :] > order[:, None]) & (before[None, :] == upto[:, None])).astype(jnp.float32)
+    behind_p = (upto[blocks - 1] == upto).astype(jnp.float32)
+    scores = jnp.where(
+        allowed[:, None], jnp.einsum("bhft,bhfs->bhts", query_blk, key_blk, precision=HIGHEST), 0.0
+    )
+    tail_keys = key_blk * block_tail[:, None, None, :]
+    tail_states = jnp.einsum("bhfs,bshe->bhfe", tail_keys, value_blk, precision=HIGHEST)
+    tail_norms = jnp.sum(tail_keys, axis=3)
+    carry_state = jnp.einsum("bc,chfe->bhfe", ahead_w, tail_states, precision=HIGHEST) + ahead_p[
+        :, None, None, None
+    ] * prefix[0][None]
+    carry_norm = jnp.einsum("bc,chf->bhf", ahead_w, tail_norms, precision=HIGHEST) + ahead_p[
+        :, None, None
+    ] * prefix[1][None]
+    numerators = jnp.einsum("bhts,bshe->bthe", scores, value_blk, precision=HIGHEST) + from_carry[
+        :, :, None, None
+    ] * jnp.einsum("bhft,bhfe->bthe", query_blk, carry_state, precision=HIGHEST)
+    denominators = jnp.sum(scores, axis=3) + from_carry[:, None, :] * jnp.einsum(
+        "bhft,bhf->bht", query_blk, carry_norm, precision=HIGHEST
+    )
     denom_rows = jnp.transpose(denominators, (0, 2, 1)).reshape(length, local_heads)
     attended = numerators.reshape(length, local_heads, HEAD_DIM) / denom_rows[:, :, None]
     grad_num = upstream / denom_rows[:, :, None]
@@ -161,59 +162,38 @@
     lead_state = jnp.einsum("hfl,lhe->hfe", lead_feat, grad_num, precision=HIGHEST)
     lead_norm = jnp.einsum("hfl,lh->hf", lead_feat, scalar_grad, precision=HIGHEST)
     suffix = carried_in(lead_state, lead_norm, jnp.zeros((0,), jnp.float32), flags, "seq", True)
-
-    def backward_block(carried, inputs):
-        back_state, back_norm = carried
-        block_index, carry_state, carry_norm, scores = inputs
-        offset_rows = block_index * block_len
-        block_start = stretch_start + offset_rows
-        query_blk = lax.dynamic_slice_in_dim(query_feat, offset_rows, block_len, 2)
-        key_blk = lax.dynamic_slice_in_dim(key_feat, offset_rows, block_len, 2)
-        value_blk = lax.dynamic_slice_in_dim(values, offset_rows, block_len, 0)
-        doc_blk = lax.dynamic_slice_in_dim(begins, offset_rows, block_len, 0)
-        grad_blk = lax.dynamic_slice_in_dim(grad_num, offset_rows, block_len, 0)
-        scalar_blk = lax.dynamic_slice_in_dim(scalar_grad, offset_rows, block_len, 0)
-        scalar_cols = scalar_blk.T
-        allowed = causal & (doc_blk[:, None] == doc_blk[None, :])
-        dscores = jnp.where(
-            allowed[None],
-            jnp.einsum("the,she->hts", grad_blk, value_blk, precision=HIGHEST)
-            + scalar_cols[:, :, None],
-            0.0,
-        )
-        from_carry = (doc_blk < block_start).astype(jnp.float32)
-        block_tail = (doc_blk == doc_blk[block_len - 1]).astype(jnp.float32)
-        carry_keep = (doc_blk[block_len - 1] < block_start).astype(jnp.float32)
-        grad_query = jnp.einsum("hts,hfs->hft", dscores, key_blk, precision=HIGHEST) + from_carry[
-            None, None, :
-        ] * (
-            jnp.einsum("hfe,the->hft", carry_state, grad_blk, precision=HIGHEST)
-            + carry_norm[:, :, None] * scalar_cols[:, None, :]
-        )
-        grad_key = jnp.einsum("hts,hft->hfs", dscores, query_blk, precision=HIGHEST) + block_tail[
-            None, None, :
-        ] * (
-            jnp.einsum("hfe,she->hfs", back_state, value_blk, precision=HIGHEST)
-            + back_norm[:, :, None]
-        )
-        grad_value = jnp.einsum("hts,the->she", scores, grad_blk, precision=HIGHEST) + block_tail[
-            :, None, None
-        ] * jnp.einsum("hfs,hfe->she", key_blk, back_state, precision=HIGHEST)
-        lead_blk = query_blk * from_carry[None, None, :]
-        next_state = (
-            jnp.einsum("hft,the->hfe", lead_blk, grad_blk, precision=HIGHEST)
-            + carry_keep * back_state
-        )
-        next_norm = (
-            jnp.einsum("hft,th->hf", lead_blk, scalar_blk, precision=HIGHEST)
-            + carry_keep * back_norm
-        )
-        return ((next_state, next_norm), (grad_query, grad_key, grad_value))
-
-    swept_back = lax.scan(
-        backward_block, (suffix[0], suffix[1]), (indices, states, norms, kept_scores), reverse=True
-    )
-    grad_qblocks, grad_kblocks, grad_vblocks = swept_back[1]
+    grad_blk = grad_num.reshape(blocks, block_len, local_heads, HEAD_DIM)
+    scalar_cols = jnp.transpose(scalar_grad.reshape(blocks, block_len, local_heads), (0, 2, 1))
+    dscores = jnp.where(
+        allowed[:, None],
+        jnp.einsum("bthe,bshe->bhts", grad_blk, value_blk, precision=HIGHEST)
+        + scalar_cols[:, :, :, None],
+        0.0,
+    )
+    lead_blk = query_blk * from_carry[:, None, None, :]
+    lead_states = jnp.einsum("bhft,bthe->bhfe", lead_blk, grad_blk, precision=HIGHEST)
+    lead_norms = jnp.einsum("bhft,bht->bhf", lead_blk, scalar_cols, precision=HIGHEST)
+    back_state = jnp.einsum("bc,chfe->bhfe", behind_w, lead_states, precision=HIGHEST) + behind_p[
+        :, None, None, None
+    ] * suffix[0][None]
+    back_norm = jnp.einsum("bc,chf->bhf", behind_w, lead_norms, precision=HIGHEST) + behind_p[
+        :, None, None
+    ] * suffix[1][None]
+    grad_qblocks = jnp.einsum("bhts,bhfs->bhft", dscores, key_blk, precision=HIGHEST) + from_carry[
+        :, None, None, :
+    ] * (
+        jnp.einsum("bhfe,bthe->bhft", carry_state, grad_blk, precision=HIGHEST)
+        + carry_norm[:, :, :, None] * scalar_cols[:, :, None, :]
+    )
+    grad_kblocks = jnp.einsum("bhts,bhft->bhfs", dscores, query_blk, precision=HIGHEST) + block_tail[
+        :, None, None, :
+    ] * (
+        jnp.einsum("bhfe,bshe->bhfs", back_state, value_blk, precision=HIGHEST)
+        + back_norm[:, :, :, None]
+    )
+    grad_vblocks = jnp.einsum("bhts,bthe->bshe", scores, grad_blk, precision=HIGHEST) + block_tail[
+        :, :, None, None
+    ] * jnp.einsum("bhfs,bhfe->bshe", key_blk, back_state, precision=HIGHEST)
     query_grad = jnp.transpose(grad_qblocks, (1, 2, 0, 3)).reshape(local_heads, feat_count, length)
     key_grad = jnp.transpose(grad_kblocks, (1, 2, 0, 3)).reshape(local_heads, feat_count, length)
     value_grad = grad_vblocks.reshape(length, local_heads, HEAD_DIM)

time: 743 us -> 539 us (0.73)
  local copies, waits for them, and re-layouts: 146 us -> 72 us
  matrix products: 117 us -> 58.9 us
  waiting for transfers between devices: 198 us -> 157 us
  loops' own time: 22.4 us -> 0 us
  other arithmetic: 85.8 us -> 74.4 us
    dot_general x112 -> x18, matrix products: 111 us -> 52.2 us  [the longest x1 5.5 us: attention_grads(): jnp.einsum('bhft,bhfs->bhts', query_blk, key_blk, precision=HIGHEST)]
    dynamic_update_slice x48 -> x0, local copies, waits for them, and re-layouts: 55 us -> none  [attention_grads(): forward_out = lax.scan(forward_block, (prefix[0], prefix[1]), indices)]
    all_gather x2, waiting for transfers between devices: 136 us -> 99.2 us  [carried_in(): gathered = lax.all_gather(padded, axis).reshape(lax.axis_size(axis), -1)]
    another operation x2 -> x0, loops' own time: 22.4 us -> none  [the longest x1 11.4 us: attention_grads(): lax.scan(backward_block, (suffix[0], suffix[1]), (indices, states, norms,...]
    dynamic_slice x24 -> x0, local copies, waits for them, and re-layouts: 9.98 us -> none  [the longest x16 9.9 us: attention_grads(): forward_out = lax.scan(forward_block, (prefix[0], prefix[1]), indices)]
    convert_element_type x32 -> x3, other arithmetic: 11.5 us -> 1.97 us  [the longest x1 1.23 us: attention_grads(): ahead_p = (before == 0).astype(jnp.float32)]
    slice x18 -> x2, local copies, waits for them, and re-layouts: 9.83 us -> 0.7 us  [the longest x1 0.52 us: attention_grads(): behind_p = (upto[blocks - 1] == upto).astype(jnp.float32)]
    unnamed x48 -> x137, local copies, waits for them, and re-layouts: 23.9 us -> 20.3 us
  transfers between devices with their start and end apart: 6 -> 6, of which waited for: 4 -> 4; matrix products, arithmetic and copies ran while one was open for 2% -> 11% of each run, Pallas kernels for 0% -> 0%
where the time goes in v2:
time: 539 us; the launch traced here: 530 us
  waiting for transfers between devices  157 us (29%)
  blocking collectives  136 us (25%)
  other arithmetic  74.4 us (14%)
  local copies, waits for them, and re-layouts  72 us (13%)
  matrix products  58.9 us (11%)
  between operations  16.3 us (3%)
  starting transfers between devices  15.7 us (3%)
    all_gather x2, waiting for transfers between devices, carried_in(): gathered = lax.all_gather(padded, axis).reshape(lax.axis_size(axis), -1)  99.2 us
    psum x1, blocking collectives, on_device(): grad_conv = lax.psum(weight_part, ('seq', 'head'))  95.5 us
    all_to_all x1, blocking collectives, on_device(): lax.all_to_all(grad_mixed, 'head', split_axis=0, concat_axis=1, tiled=True)  40.9 us
    all_to_all x1, waiting for transfers between devices, on_device(): lax.all_to_all(outgoing, 'head', split_axis=1, concat_axis=0, tiled=True)  32.7 us
    all_to_all x1, waiting for transfers between devices, on_device(): lax.all_to_all(out_grads, 'head', split_axis=1, concat_axis=0, tiled=True)  24.8 us
    unnamed x137, local copies, waits for them, and re-layouts  20.3 us
    scatter-add x2, other arithmetic, feature_map(): columns[:, upper_i, :] * columns[:, upper_j, :]  15.1 us
    scatter-add x2, other arithmetic, feature_map(): columns[:, upper_j, :]  14.9 us
  transfers between devices with their start and end apart: 6, of which 4 were waited for; matrix products, arithmetic and copies ran while one was open for 11% of the time, Pallas kernels for 0%

profile of v2, /device:TPU:1, one launch (start us, length us, event | category | flops | bytes accessed | tf_op | source)
XLA Modules:
  0.0 530.4 jit_solution(4699132268931788795)
XLA Ops:
  8.1 4.0 collective-permute-start
  17.7 3.1 multiply_add_fusion
  20.8 6.1 %all-to-all-start = ((f32[128,8,320]{0,2,1:T(8,128)}), f32[128,8,320]{0,2,1:T(8,128)S(1)}, u32[]{:S(2)}, u32[]{:S(2)}) async-start(f32[128,8,320]{0,2,1:T(8,128)} %bitcast.230), calls=%async_computation | async-start | bytes 2621440 | tf_op jit(solution)/shard_map/all_to_all | solution.py:219
  29.0 32.7 %all-to-all-done = f32[128,8,320]{0,2,1:T(8,128)S(1)} async-done(((f32[128,8,320]{0,2,1:T(8,128)}), f32[128,8,320]{0,2,1:T(8,128)S(1)}, u32[]{:S(2)}, u32[]{:S(2)}) %all-to-all-start) | async-done | bytes 1310752 | tf_op jit(solution)/shard_map/all_to_all | solution.py:219
  64.6 3.1 gather_fusion.1
  67.7 3.0 gather_fusion.2
  70.7 3.0 gather_fusion.3
  73.8 3.1 fusion.51
  76.9 4.5 fusion.101
  85.3 3.6 all-to-all-start.1
  93.2 24.8 %all-to-all-done.1 = f32[128,8,256]{0,2,1:T(8,128)S(1)} async-done(((f32[128,8,256]{0,2,1:T(8,128)}), f32[128,8,256]{0,2,1:T(8,128)S(1)}, u32[]{:S(2)}, u32[]{:S(2)}) %all-to-all-start.1) | async-done | bytes 1048608 | tf_op jit(solution)/shard_map/all_to_all | solution.py:220
  129.2 3.4 fusion.39
  132.6 5.5 %fusion.102 = (f32[8,2,128]{2,1,0:T(2,128)}, f32[8,2,128,128]{2,3,1,0:T(8,128)}) fusion(f32[2,153,8,128]{3,2,0,1:T(8,128)S(1)} %reshape.454, f32[2,153,8,128]{3,2,0,1:T(8,128)S(1)} %reshape.455, pred[8,128,128]{1,2,0:T(8,128)(4,1)S(1)} %copy-done.29), kind=kOutput, calls=%fused_computation.199 | convolution fusion | flops 481818624 | bytes 3694592 | tf_op jit(solution)/shard_map/bhft,bhfs->bhts/dot_general | solution.py:139
  138.1 37.5 %all-gather.3.cloned.1.call-done = f32[64,309,128]{2,1,0:T(8,128)} async-done(((f32[1,309,128]{2,1,0:T(8,128)}), f32[64,309,128]{2,1,0:T(8,128)}) %all-gather.3.cloned.1.call-update) | async-done | bytes 10125328 | tf_op jit(solution)/shard_map/all_gather | solution.py:35
  175.6 5.7 %copy.490 = f32[8,8,309,128]{3,1,2,0:T(8,128)S(1)} copy(f32[8,8,309,128]{3,2,1,0:T(8,128)} %bitcast.223) | data formatting | bytes 20250624
  189.6 4.3 convolution_multiply_fusion.1
  233.8 3.7 fusion.41
  237.4 3.7 convolution_bitcast_fusion.1
  241.1 3.7 fusion.42
  244.8 61.7 %all-gather.5.cloned.1.call-done = f32[64,309,128]{2,1,0:T(8,128)} async-done(((f32[1,309,128]{2,1,0:T(8,128)}), f32[64,309,128]{2,1,0:T(8,128)}) %all-gather.5.cloned.1.call-update) | async-done | bytes 10125328 | tf_op jit(solution)/shard_map/all_gather | solution.py:35
  306.5 5.7 %copy.489 = f32[8,8,309,128]{3,1,2,0:T(8,128)S(1)} copy(f32[8,8,309,128]{3,2,1,0:T(8,128)} %bitcast.224) | data formatting | bytes 20250624
  320.9 2.9 reshape.457
  323.8 5.7 %fusion.47 = (f32[136,2,1024]{2,1,0:T(2,128)}, f32[136,2,1024]{2,1,0:T(2,128)}, f32[136,2,1024]{2,1,0:T(2,128)}, f32[136,2,1024]{2,1,0:T(2,128)}) fusion(f32[136,2,1024]{2,1,0:T(2,128)} %gather_fusion.3, f32[2,153,1024]{2,0,1:T(2,128)S(1)} %copy-done, f32[136]{0:T(256)S(1)} %copy-done.58, f32[136,2,1024]{2,1,0:T(2,128)} %gather_fusion.2, ...), kind=kLoop, calls=%fused_computation.90 | loop fusion | flops 1671168 | bytes 11141664 | tf_op jit(solution)/shard_map/transpose(jvp())/mul | solution.py:52
  329.5 4.8 convolution_multiply_fusion
  334.3 7.3 %scatter_fusion = f32[2,16,1024]{2,0,1:T(2,128)S(1)} fusion(f32[2,16,1024]{2,0,1:T(2,128)S(1)} %slice-done, s32[136]{0:T(256)S(1)} %copy-done.48, f32[136,2,1024]{2,1,0:T(2,128)S(1)} %copy-done.22), kind=kCustom, calls=%fused_computation.4 | custom fusion | flops 278528 | bytes 3342880 | tf_op jit(solution)/shard_map/transpose(jvp())/scatter-add | solution.py:52
  341.8 7.6 %scatter_fusion.1 = f32[2,16,1024]{2,0,1:T(2,128)S(1)} fusion(f32[2,16,1024]{2,0,1:T(2,128)S(1)} %broadcast.223.clone.1, s32[136]{0:T(256)S(1)} %copy-done.50, f32[136,2,1024]{2,1,0:T(2,128)S(1)} %copy-done.21), kind=kCustom, calls=%fused_computation.5 | custom fusion | flops 278528 | bytes 3342880 | tf_op jit(solution)/shard_map/transpose(jvp())/scatter-add | solution.py:52
  350.9 7.6 %scatter_fusion.3 = f32[2,16,1024]{2,0,1:T(2,128)S(1)} fusion(f32[2,16,1024]{2,0,1:T(2,128)S(1)} %broadcast.223.clone, s32[136]{0:T(256)S(1)} %copy-done.50, f32[136,2,1024]{2,1,0:T(2,128)S(1)} %copy-done.20), kind=kCustom, calls=%fused_computation.7 | custom fusion | flops 278528 | bytes 3342880 | tf_op jit(solution)/shard_map/transpose(jvp())/scatter-add | solution.py:52
  358.5 7.6 %scatter_fusion.2 = f32[2,16,1024]{2,0,1:T(2,128)S(1)} fusion(f32[2,16,1024]{2,0,1:T(2,128)S(1)} %slice-done.1, s32[136]{0:T(256)S(1)} %copy-done.48, f32[136,2,1024]{2,1,0:T(2,128)S(1)} %copy-done.19), kind=kCustom, calls=%fused_computation.6 | custom fusion | flops 278528 | bytes 3342880 | tf_op jit(solution)/shard_map/transpose(jvp())/scatter-add | solution.py:52
  367.3 3.5 fusion.8
  374.6 40.9 %all_to_all.51 = f32[8,128,320]{1,2,0:T(8,128)S(1)} all-to-all(f32[8,128,320]{1,2,0:T(8,128)S(1)} %copy.363), channel_id=1, replica_groups=mesh['seq'=64,'head'=8] {'head'}, dimensions={0} | all-to-all | bytes 2621440 | tf_op jit(solution)/shard_map/all_to_all | solution.py:224
  420.2 95.5 %psum.7 = f32[3,2560]{1,0:T(4,128)} all-reduce(f32[3,2560]{1,0:T(4,128)S(1)} %pad_maximum_fusion.5), channel_id=1, replica_groups=mesh['seq'=64,'head'=8] {'seq','head'}, use_global_device_ids=true, to_apply=%region_19.20 | all-reduce | flops 7680 | bytes 61440 | tf_op jit(solution)/shard_map/psum | solution.py:229
  517.2 4.4 fusion.15
  (250 shorter events, 100.5 us)
Async XLA Ops:
  8.1 9.1 %collective-permute-start = (f32[2,2560]{1,0:T(2,128)S(1)}, f32[2,2560]{1,0:T(2,128)S(1)}, u32[]{:S(2)}, u32[]{:S(2)}) collective-permute-start(f32[2,2560]{1,0:T(2,128)S(1)} %slice.110), channel_id=1, source_target_pairs={{0,1},{1,2},{2,3},{3,4},{4,5},{5,6},{6,7},{7,8},{8,9},{9,10},{10,1... | collective-permute-start | bytes 61448 | tf_op jit(solution)/shard_map/ppermute | solution.py:45
  20.8 7.5 %copy-start.49 = (s32[136]{0:T(256)S(1)}, s32[136]{0:T(256)}, u32[]{:S(2)}) copy-start(s32[136]{0:T(256)} %constant.67) | copy-start | bytes 1636
  20.8 7.5 %copy-start.47 = (s32[136]{0:T(256)S(1)}, s32[136]{0:T(256)}, u32[]{:S(2)}) copy-start(s32[136]{0:T(256)} %constant.68) | copy-start | bytes 1636
  20.8 40.9 %all-to-all-start = ((f32[128,8,320]{0,2,1:T(8,128)}), f32[128,8,320]{0,2,1:T(8,128)S(1)}, u32[]{:S(2)}, u32[]{:S(2)}) async-start(f32[128,8,320]{0,2,1:T(8,128)} %bitcast.230), calls=%async_computation | async-start | bytes 2621440 | tf_op jit(solution)/shard_map/all_to_all | solution.py:219
  26.8 148.8 %all-gather.3.cloned.1.call-start = ((), (), s32[]{:S(2)}) async-start(), calls=%async_computation.3 | async-start | bytes 10383360 | tf_op jit(solution)/shard_map/all_gather | solution.py:35
  62.6 59.4 %copy-start.7 = (f32[1024,2,160]{0,2,1:T(8,128)}, f32[1024,2,160]{0,2,1:T(8,128)S(1)}, u32[]{:S(2)}) copy-start(f32[1024,2,160]{0,2,1:T(8,128)S(1)} %reshape.360) | copy-start | bytes 3932164
  64.6 9.1 %copy-start.8 = (f32[136,2,1024]{2,1,0:T(2,128)}, f32[136,2,1024]{2,1,0:T(2,128)S(1)}, u32[]{:S(2)}) copy-start(f32[136,2,1024]{2,1,0:T(2,128)S(1)} %gather_fusion) | copy-start | bytes 3342340
  85.3 32.7 %all-to-all-start.1 = ((f32[128,8,256]{0,2,1:T(8,128)}), f32[128,8,256]{0,2,1:T(8,128)S(1)}, u32[]{:S(2)}, u32[]{:S(2)}) async-start(f32[128,8,256]{0,2,1:T(8,128)} %bitcast.235), calls=%async_computation.1 | async-start | bytes 2097152 | tf_op jit(solution)/shard_map/all_to_all | solution.py:220
  88.8 217.6 %all-gather.5.cloned.1.call-start = ((), (), s32[]{:S(2)}) async-start(), calls=%async_computation.4 | async-start | bytes 10383360 | tf_op jit(solution)/shard_map/all_gather | solution.py:35
  90.5 31.5 %copy-start.51 = (s32[8]{0:T(128)}, s32[8]{0:T(128)S(1)}, u32[]{:S(2)}) copy-start(s32[8]{0:T(128)S(1)} %get-tuple-element.21) | copy-start | bytes 100
  189.5 4.4 copy-start.16
  231.8 5.6 %copy-start.24 = (f32[8,2,128,128]{2,3,1,0:T(8,128)S(1)}, f32[8,2,128,128]{2,3,1,0:T(8,128)}, u32[]{:S(2)}) copy-start(f32[8,2,128,128]{2,3,1,0:T(8,128)} %copy-done.23) | copy-start | bytes 3145732
  306.5 5.7 %copy-start.63 = (pred[64]{0:T(512)(128)(4,1)S(1)}, pred[64]{0:T(512)(128)(4,1)}, u32[]{:S(2)}) copy-start(pred[64]{0:T(512)(128)(4,1)} %compare_and_fusion.1) | copy-start | bytes 196
  323.8 5.7 %copy-start.2 = (f32[8,2,153,128]{3,0,2,1:T(8,128)S(1)}, f32[8,2,153,128]{3,0,2,1:T(8,128)}, u32[]{:S(2)}) copy-start(f32[8,2,153,128]{3,0,2,1:T(8,128)} %copy-done.1) | copy-start | bytes 3760132
  329.4 4.9 slice-start
  329.5 4.9 copy-start.22
  329.5 4.8 copy-start.48
  334.3 7.4 %copy-start.21 = (f32[136,2,1024]{2,1,0:T(2,128)S(1)}, f32[136,2,1024]{2,1,0:T(2,128)}, u32[]{:S(2)}) copy-start(f32[136,2,1024]{2,1,0:T(2,128)} %get-tuple-element.33) | copy-start | bytes 3342340
  334.3 7.4 %copy-start.50 = (s32[136]{0:T(256)S(1)}, s32[136]{0:T(256)}, u32[]{:S(2)}) copy-start(s32[136]{0:T(256)} %constant.67) | copy-start | bytes 1636
  350.9 7.6 %slice-start.1 = ((f32[2,153,1024]{2,0,1:T(2,128)}), f32[2,16,1024]{2,0,1:T(2,128)S(1)}, s32[]{:S(2)}) async-start(f32[2,153,1024]{2,0,1:T(2,128)} %reshape.457), calls=%async_computation.6 | async-start | bytes 262144 | tf_op jit(solution)/shard_map/transpose(jvp())/split | solution.py:54
  350.9 7.6 %copy-start.19 = (f32[136,2,1024]{2,1,0:T(2,128)S(1)}, f32[136,2,1024]{2,1,0:T(2,128)}, u32[]{:S(2)}) copy-start(f32[136,2,1024]{2,1,0:T(2,128)} %get-tuple-element.45) | copy-start | bytes 3342340
  358.5 8.1 %copy-start.14 = (f32[8,2,128,128]{2,3,1,0:T(8,128)S(1)}, f32[8,2,128,128]{2,3,1,0:T(8,128)}, u32[]{:S(2)}) copy-start(f32[8,2,128,128]{2,3,1,0:T(8,128)} %get-tuple-element.53) | copy-start | bytes 3145732
  374.3 41.2 %copy-start.54 = (f32[128]{0:T(128)S(1)}, f32[128]{0:T(128)}, u32[]{:S(2)}) copy-start(f32[128]{0:T(128)} %copy-done.53) | copy-start | bytes 1540
  374.3 41.2 %copy-start.56 = (f32[128]{0:T(128)S(1)}, f32[128]{0:T(128)}, u32[]{:S(2)}) copy-start(f32[128]{0:T(128)} %copy-done.55) | copy-start | bytes 1540
  374.6 41.0 %copy-start.4 = (f32[128,2560]{0,1:T(8,128)S(1)}, f32[128,2560]{0,1:T(8,128)}, u32[]{:S(2)}) copy-start(f32[128,2560]{0,1:T(8,128)} %copy-done.3) | copy-start | bytes 3932164
  374.6 41.0 %copy-start.6 = (f32[2,2560]{0,1:T(8,128)S(1)}, f32[2,2560]{0,1:T(8,128)}, u32[]{:S(2)}) copy-start(f32[2,2560]{0,1:T(8,128)} %copy-done.5) | copy-start | bytes 61444
  417.8 99.4 %copy-start.35 = (f32[2560]{0:T(1024)S(1)}, f32[2560]{0:T(1024)}, u32[]{:S(2)}) copy-start(f32[2560]{0:T(1024)} %copy-done.34) | copy-start | bytes 30724
  417.8 99.4 %copy-start.37 = (f32[2560]{0:T(1024)S(1)}, f32[2560]{0:T(1024)}, u32[]{:S(2)}) copy-start(f32[2560]{0:T(1024)} %copy-done.36) | copy-start | bytes 30724
  417.8 99.4 %copy-start.39 = (f32[2560]{0:T(1024)S(1)}, f32[2560]{0:T(1024)}, u32[]{:S(2)}) copy-start(f32[2560]{0:T(1024)} %copy-done.38) | copy-start | bytes 30724
  417.8 99.4 %copy-start.59 = (f32[128]{0:T(128)S(1)}, f32[128]{0:T(128)}, u32[]{:S(2)}) copy-start(f32[128]{0:T(128)} %get-tuple-element.41) | copy-start | bytes 1540
  417.8 99.4 %copy-start.60 = (f32[128]{0:T(128)S(1)}, f32[128]{0:T(128)}, u32[]{:S(2)}) copy-start(f32[128]{0:T(128)} %get-tuple-element.43) | copy-start | bytes 1540
  418.2 97.5 %collective-permute-start.1 = (f32[2,2560]{1,0:T(2,128)S(1)}, f32[2,2560]{1,0:T(2,128)S(1)}, u32[]{:S(2)}, u32[]{:S(2)}) collective-permute-start(f32[2,2560]{1,0:T(2,128)S(1)} %copy.364), channel_id=1, source_target_pairs={{1,0},{2,1},{3,2},{4,3},{5,4},{6,5},{7,6},{8,7},{9,8},{10,9},{11,1... | collective-permute-start | bytes 61448 | tf_op jit(solution)/shard_map/ppermute | solution.py:45
  (41 other events, 103.0 us)
Sparse Core Ops, SparseCore 0:
  84.1 91.5 all-gather.2
  217.9 88.5 all-gather.4

commit v3 on v2

--- a/solution.py
+++ b/solution.py
@@ -204,6 +204,13 @@
     )
 
 
+def summed_everywhere(part):
+    head_count = lax.axis_size("head")
+    mine = lax.psum_scatter(part, "head", scatter_dimension=1, tiled=True)
+    total = jnp.sum(lax.all_gather(mine, "seq"), axis=0)
+    return lax.all_gather(total, "head", axis=1, tiled=True)
+
+
 def on_device(projected, out_grads, conv_weight, doc_lengths):
     row_count = projected.shape[0]
     head_count = lax.axis_size("head")
@@ -226,7 +233,7 @@
     grad_projected, weight_part = conv_backward(
         returned, trailing, projected, leading, conv_weight, token_offsets
     )
-    grad_conv = lax.psum(weight_part, ("seq", "head"))
+    grad_conv = summed_everywhere(weight_part)
     return (grad_projected, grad_conv)
 
 

time: 539 us -> 550 us (1.020)
  the two profiles are of different devices: /device:TPU:1 before, /device:TPU:24 now
where the time goes in v3:
time: 550 us; the launch traced here: 541 us
  waiting for transfers between devices  181 us (33%)
  blocking collectives  114 us (21%)
  local copies, waits for them, and re-layouts  75.4 us (14%)
  other arithmetic  74.5 us (14%)
  matrix products  58.7 us (11%)
  starting transfers between devices  21.1 us (4%)
  between operations  15.9 us (3%)
    all_gather x2, waiting for transfers between devices, carried_in(): gathered = lax.all_gather(padded, axis).reshape(lax.axis_size(axis), -1)  103 us
    all_gather x1, blocking collectives, summed_everywhere(): total = jnp.sum(lax.all_gather(mine, 'seq'), axis=0)  50.9 us
    all_to_all x1, blocking collectives, on_device(): lax.all_to_all(grad_mixed, 'head', split_axis=0, concat_axis=1, tiled=True)  38.3 us
    unnamed x4, waiting for transfers between devices  28.1 us
    all_to_all x1, waiting for transfers between devices, on_device(): lax.all_to_all(outgoing, 'head', split_axis=1, concat_axis=0, tiled=True)  27.5 us
    all_gather x1, blocking collectives, summed_everywhere(): return lax.all_gather(total, 'head', axis=1, tiled=True)  24.6 us
    unnamed x140, local copies, waits for them, and re-layouts  23.5 us
    all_to_all x1, waiting for transfers between devices, on_device(): lax.all_to_all(out_grads, 'head', split_axis=1, concat_axis=0, tiled=True)  20.6 us
  transfers between devices with their start and end apart: 7, of which 6 were waited for; matrix products, arithmetic and copies ran while one was open for 12% of the time, Pallas kernels for 0%

profile of v3, /device:TPU:24, one launch (start us, length us, event | category | flops | bytes accessed | tf_op | source)
XLA Modules:
  0.0 540.7 jit_solution(16019431382526466041)
XLA Ops:
  8.1 4.7 collective-permute-start
  18.3 3.1 multiply_add_fusion
  21.4 5.8 %all-to-all-start = ((f32[128,8,320]{0,2,1:T(8,128)}), f32[128,8,320]{0,2,1:T(8,128)S(1)}, u32[]{:S(2)}, u32[]{:S(2)}) async-start(f32[128,8,320]{0,2,1:T(8,128)} %bitcast.239), calls=%async_computation | async-start | bytes 2621440 | tf_op jit(solution)/shard_map/all_to_all | solution.py:226
  29.3 27.5 %all-to-all-done = f32[128,8,320]{0,2,1:T(8,128)S(1)} async-done(((f32[128,8,320]{0,2,1:T(8,128)}), f32[128,8,320]{0,2,1:T(8,128)S(1)}, u32[]{:S(2)}, u32[]{:S(2)}) %all-to-all-start) | async-done | bytes 1310752 | tf_op jit(solution)/shard_map/all_to_all | solution.py:226
  59.8 3.1 gather_fusion.1
  65.9 3.0 gather_fusion.3
  69.0 3.1 fusion.51
  72.1 4.5 fusion.101
  80.5 7.5 %all-to-all-start.1 = ((f32[128,8,256]{0,2,1:T(8,128)}), f32[128,8,256]{0,2,1:T(8,128)S(1)}, u32[]{:S(2)}, u32[]{:S(2)}) async-start(f32[128,8,256]{0,2,1:T(8,128)} %bitcast.245), calls=%async_computation.1 | async-start | bytes 2097152 | tf_op jit(solution)/shard_map/all_to_all | solution.py:227
  92.3 20.6 %all-to-all-done.1 = f32[128,8,256]{0,2,1:T(8,128)S(1)} async-done(((f32[128,8,256]{0,2,1:T(8,128)}), f32[128,8,256]{0,2,1:T(8,128)S(1)}, u32[]{:S(2)}, u32[]{:S(2)}) %all-to-all-start.1) | async-done | bytes 1048608 | tf_op jit(solution)/shard_map/all_to_all | solution.py:227
  124.1 3.4 fusion.39
  127.6 5.5 %fusion.102 = (f32[8,2,128]{2,1,0:T(2,128)}, f32[8,2,128,128]{2,3,1,0:T(8,128)}) fusion(f32[2,153,8,128]{3,2,0,1:T(8,128)S(1)} %reshape.460, f32[2,153,8,128]{3,2,0,1:T(8,128)S(1)} %reshape.461, pred[8,128,128]{1,2,0:T(8,128)(4,1)S(1)} %copy-done.29), kind=kOutput, calls=%fused_computation.199 | convolution fusion | flops 481818624 | bytes 3694592 | tf_op jit(solution)/shard_map/bhft,bhfs->bhts/dot_general | solution.py:139
  133.1 41.0 %all-gather.6.cloned.1.call-done = f32[64,309,128]{2,1,0:T(8,128)} async-done(((f32[1,309,128]{2,1,0:T(8,128)}), f32[64,309,128]{2,1,0:T(8,128)}) %all-gather.6.cloned.1.call-update) | async-done | bytes 10125328 | tf_op jit(solution)/shard_map/all_gather | solution.py:35
  174.1 5.7 %copy.494 = f32[8,8,309,128]{3,1,2,0:T(8,128)S(1)} copy(f32[8,8,309,128]{3,2,1,0:T(8,128)} %bitcast.232) | data formatting | bytes 20250624
  188.0 4.3 convolution_multiply_fusion.1
  232.2 3.7 fusion.41
  235.9 3.7 convolution_bitcast_fusion.1
  239.6 3.7 fusion.42
  243.2 61.7 %all-gather.8.cloned.1.call-done = f32[64,309,128]{2,1,0:T(8,128)} async-done(((f32[1,309,128]{2,1,0:T(8,128)}), f32[64,309,128]{2,1,0:T(8,128)}) %all-gather.8.cloned.1.call-update) | async-done | bytes 10125328 | tf_op jit(solution)/shard_map/all_gather | solution.py:35
  305.0 5.7 %copy.493 = f32[8,8,309,128]{3,1,2,0:T(8,128)S(1)} copy(f32[8,8,309,128]{3,2,1,0:T(8,128)} %bitcast.233) | data formatting | bytes 20250624
  322.3 5.7 %fusion.47 = (f32[136,2,1024]{2,1,0:T(2,128)}, f32[136,2,1024]{2,1,0:T(2,128)}, f32[136,2,1024]{2,1,0:T(2,128)}, f32[136,2,1024]{2,1,0:T(2,128)}) fusion(f32[136,2,1024]{2,1,0:T(2,128)} %gather_fusion.3, f32[2,153,1024]{2,0,1:T(2,128)S(1)} %copy-done, f32[136]{0:T(256)S(1)} %copy-done.58, f32[136,2,1024]{2,1,0:T(2,128)} %gather_fusion.2, ...), kind=kLoop, calls=%fused_computation.90 | loop fusion | flops 1671168 | bytes 11141664 | tf_op jit(solution)/shard_map/transpose(jvp())/mul | solution.py:52
  328.0 4.8 convolution_multiply_fusion
  332.8 7.3 %scatter_fusion = f32[2,16,1024]{2,0,1:T(2,128)S(1)} fusion(f32[2,16,1024]{2,0,1:T(2,128)S(1)} %slice-done, s32[136]{0:T(256)S(1)} %copy-done.48, f32[136,2,1024]{2,1,0:T(2,128)S(1)} %copy-done.22), kind=kCustom, calls=%fused_computation.4 | custom fusion | flops 278528 | bytes 3342880 | tf_op jit(solution)/shard_map/transpose(jvp())/scatter-add | solution.py:52
  340.2 7.6 %scatter_fusion.1 = f32[2,16,1024]{2,0,1:T(2,128)S(1)} fusion(f32[2,16,1024]{2,0,1:T(2,128)S(1)} %broadcast.223.clone.1, s32[136]{0:T(256)S(1)} %copy-done.50, f32[136,2,1024]{2,1,0:T(2,128)S(1)} %copy-done.21), kind=kCustom, calls=%fused_computation.5 | custom fusion | flops 278528 | bytes 3342880 | tf_op jit(solution)/shard_map/transpose(jvp())/scatter-add | solution.py:52
  349.4 7.6 %scatter_fusion.3 = f32[2,16,1024]{2,0,1:T(2,128)S(1)} fusion(f32[2,16,1024]{2,0,1:T(2,128)S(1)} %broadcast.223.clone, s32[136]{0:T(256)S(1)} %copy-done.50, f32[136,2,1024]{2,1,0:T(2,128)S(1)} %copy-done.20), kind=kCustom, calls=%fused_computation.7 | custom fusion | flops 278528 | bytes 3342880 | tf_op jit(solution)/shard_map/transpose(jvp())/scatter-add | solution.py:52
  357.0 7.6 %scatter_fusion.2 = f32[2,16,1024]{2,0,1:T(2,128)S(1)} fusion(f32[2,16,1024]{2,0,1:T(2,128)S(1)} %slice-done.1, s32[136]{0:T(256)S(1)} %copy-done.48, f32[136,2,1024]{2,1,0:T(2,128)S(1)} %copy-done.19), kind=kCustom, calls=%fused_computation.6 | custom fusion | flops 278528 | bytes 3342880 | tf_op jit(solution)/shard_map/transpose(jvp())/scatter-add | solution.py:52
  365.8 3.5 fusion.8
  373.1 38.3 %all_to_all.51 = f32[8,128,320]{1,2,0:T(8,128)S(1)} all-to-all(f32[8,128,320]{1,2,0:T(8,128)S(1)} %copy.364), channel_id=1, replica_groups=mesh['seq'=64,'head'=8] {'head'}, dimensions={0} | all-to-all | bytes 2621440 | tf_op jit(solution)/shard_map/all_to_all | solution.py:231
  422.4 4.4 fusion.15
  428.3 28.1 %reduce-scatter.4.cloned.1.call-done = f32[320,3]{1,0:T(8,128)} async-done(((f32[2560,3]{1,0:T(8,128)}), f32[320,3]{1,0:T(8,128)}) %reduce-scatter.4.cloned.1.call-update) | async-done | bytes 3856
  457.4 50.9 %all-gather.1 = f32[64,3,320]{2,1,0:T(4,128)S(1)} all-gather(f32[1,3,320]{2,1,0:T(4,128)S(1)} %bitcast.260), channel_id=2, replica_groups=mesh['seq'=64,'head'=8] {'seq'}, dimensions={0}, use_global_device_ids=true | all-gather | bytes 249600 | tf_op jit(solution)/shard_map/all_gather | solution.py:210
  508.4 24.6 %all-gather.2 = f32[8,320,3]{1,2,0:T(4,128)S(1)} all-gather(f32[1,320,3]{1,2,0:T(4,128)S(1)} %bitcast.259), channel_id=1, replica_groups=mesh['seq'=64,'head'=8] {'head'}, dimensions={0}, use_global_device_ids=true | all-gather | bytes 34560 | tf_op jit(solution)/shard_map/all_gather | solution.py:211
  (259 shorter events, 113.1 us)
Async XLA Ops:
  8.1 9.8 %collective-permute-start = (f32[2,2560]{1,0:T(2,128)S(1)}, f32[2,2560]{1,0:T(2,128)S(1)}, u32[]{:S(2)}, u32[]{:S(2)}) collective-permute-start(f32[2,2560]{1,0:T(2,128)S(1)} %slice.110), channel_id=1, source_target_pairs={{0,1},{1,2},{2,3},{3,4},{4,5},{5,6},{6,7},{7,8},{8,9},{9,10},{10,1... | collective-permute-start | bytes 61448 | tf_op jit(solution)/shard_map/ppermute | solution.py:45
  21.4 7.2 %copy-start.49 = (s32[136]{0:T(256)S(1)}, s32[136]{0:T(256)}, u32[]{:S(2)}) copy-start(s32[136]{0:T(256)} %constant.67) | copy-start | bytes 1636
  21.4 7.2 %copy-start.47 = (s32[136]{0:T(256)S(1)}, s32[136]{0:T(256)}, u32[]{:S(2)}) copy-start(s32[136]{0:T(256)} %constant.68) | copy-start | bytes 1636
  21.4 35.4 %all-to-all-start = ((f32[128,8,320]{0,2,1:T(8,128)}), f32[128,8,320]{0,2,1:T(8,128)S(1)}, u32[]{:S(2)}, u32[]{:S(2)}) async-start(f32[128,8,320]{0,2,1:T(8,128)} %bitcast.239), calls=%async_computation | async-start | bytes 2621440 | tf_op jit(solution)/shard_map/all_to_all | solution.py:226
  27.3 146.8 %all-gather.6.cloned.1.call-start = ((), (), s32[]{:S(2)}) async-start(), calls=%async_computation.4 | async-start | bytes 10383360 | tf_op jit(solution)/shard_map/all_gather | solution.py:35
  57.8 59.1 %copy-start.7 = (f32[1024,2,160]{0,2,1:T(8,128)}, f32[1024,2,160]{0,2,1:T(8,128)S(1)}, u32[]{:S(2)}) copy-start(f32[1024,2,160]{0,2,1:T(8,128)S(1)} %reshape.360) | copy-start | bytes 3932164
  59.8 9.1 %copy-start.8 = (f32[136,2,1024]{2,1,0:T(2,128)}, f32[136,2,1024]{2,1,0:T(2,128)S(1)}, u32[]{:S(2)}) copy-start(f32[136,2,1024]{2,1,0:T(2,128)S(1)} %gather_fusion) | copy-start | bytes 3342340
  80.5 32.5 %all-to-all-start.1 = ((f32[128,8,256]{0,2,1:T(8,128)}), f32[128,8,256]{0,2,1:T(8,128)S(1)}, u32[]{:S(2)}, u32[]{:S(2)}) async-start(f32[128,8,256]{0,2,1:T(8,128)} %bitcast.245), calls=%async_computation.1 | async-start | bytes 2097152 | tf_op jit(solution)/shard_map/all_to_all | solution.py:227
  88.0 217.0 %all-gather.8.cloned.1.call-start = ((), (), s32[]{:S(2)}) async-start(), calls=%async_computation.5 | async-start | bytes 10383360 | tf_op jit(solution)/shard_map/all_gather | solution.py:35
  89.5 27.4 %copy-start.51 = (s32[8]{0:T(128)}, s32[8]{0:T(128)S(1)}, u32[]{:S(2)}) copy-start(s32[8]{0:T(128)S(1)} %get-tuple-element.21) | copy-start | bytes 100
  112.9 4.0 copy-start.9
  188.0 4.4 copy-start.16
  188.0 4.4 copy-start.13
  199.3 3.9 copy-start.45
  199.3 3.9 copy-start.26
  216.3 240.1 %reduce-scatter.4.cloned.1.call-start = ((), (), s32[]{:S(2)}) async-start(), calls=%async_computation.6 | async-start | bytes 1474560
  230.3 5.7 %copy-start.24 = (f32[8,2,128,128]{2,3,1,0:T(8,128)S(1)}, f32[8,2,128,128]{2,3,1,0:T(8,128)}, u32[]{:S(2)}) copy-start(f32[8,2,128,128]{2,3,1,0:T(8,128)} %copy-done.23) | copy-start | bytes 3145732
  305.0 5.7 %copy-start.63 = (pred[64]{0:T(512)(128)(4,1)S(1)}, pred[64]{0:T(512)(128)(4,1)}, u32[]{:S(2)}) copy-start(pred[64]{0:T(512)(128)(4,1)} %compare_and_fusion.1) | copy-start | bytes 196
  322.3 5.7 %copy-start.2 = (f32[8,2,153,128]{3,0,2,1:T(8,128)S(1)}, f32[8,2,153,128]{3,0,2,1:T(8,128)}, u32[]{:S(2)}) copy-start(f32[8,2,153,128]{3,0,2,1:T(8,128)} %copy-done.1) | copy-start | bytes 3760132
  327.9 4.9 slice-start
  327.9 4.9 copy-start.22
  328.0 4.8 copy-start.48
  332.8 7.4 %copy-start.21 = (f32[136,2,1024]{2,1,0:T(2,128)S(1)}, f32[136,2,1024]{2,1,0:T(2,128)}, u32[]{:S(2)}) copy-start(f32[136,2,1024]{2,1,0:T(2,128)} %get-tuple-element.33) | copy-start | bytes 3342340
  332.8 7.4 %copy-start.50 = (s32[136]{0:T(256)S(1)}, s32[136]{0:T(256)}, u32[]{:S(2)}) copy-start(s32[136]{0:T(256)} %constant.67) | copy-start | bytes 1636
  349.4 7.6 %slice-start.1 = ((f32[2,153,1024]{2,0,1:T(2,128)}), f32[2,16,1024]{2,0,1:T(2,128)S(1)}, s32[]{:S(2)}) async-start(f32[2,153,1024]{2,0,1:T(2,128)} %reshape.465), calls=%async_computation.8 | async-start | bytes 262144 | tf_op jit(solution)/shard_map/transpose(jvp())/split | solution.py:54
  349.4 7.6 %copy-start.19 = (f32[136,2,1024]{2,1,0:T(2,128)S(1)}, f32[136,2,1024]{2,1,0:T(2,128)}, u32[]{:S(2)}) copy-start(f32[136,2,1024]{2,1,0:T(2,128)} %get-tuple-element.45) | copy-start | bytes 3342340
  357.0 8.1 %copy-start.14 = (f32[8,2,128,128]{2,3,1,0:T(8,128)S(1)}, f32[8,2,128,128]{2,3,1,0:T(8,128)}, u32[]{:S(2)}) copy-start(f32[8,2,128,128]{2,3,1,0:T(8,128)} %get-tuple-element.53) | copy-start | bytes 3145732
  372.8 38.6 %copy-start.54 = (f32[128]{0:T(128)S(1)}, f32[128]{0:T(128)}, u32[]{:S(2)}) copy-start(f32[128]{0:T(128)} %copy-done.53) | copy-start | bytes 1540
  372.8 38.6 %copy-start.56 = (f32[128]{0:T(128)S(1)}, f32[128]{0:T(128)}, u32[]{:S(2)}) copy-start(f32[128]{0:T(128)} %copy-done.55) | copy-start | bytes 1540
  373.1 38.4 %copy-start.4 = (f32[128,2560]{0,1:T(8,128)S(1)}, f32[128,2560]{0,1:T(8,128)}, u32[]{:S(2)}) copy-start(f32[128,2560]{0,1:T(8,128)} %copy-done.3) | copy-start | bytes 3932164
  373.1 38.4 %copy-start.6 = (f32[2,2560]{0,1:T(8,128)S(1)}, f32[2,2560]{0,1:T(8,128)}, u32[]{:S(2)}) copy-start(f32[2,2560]{0,1:T(8,128)} %copy-done.5) | copy-start | bytes 61444
  414.0 6.9 %collective-permute-start.1 = (f32[2,2560]{1,0:T(2,128)S(1)}, f32[2,2560]{1,0:T(2,128)S(1)}, u32[]{:S(2)}, u32[]{:S(2)}) collective-permute-start(f32[2,2560]{1,0:T(2,128)S(1)} %copy.365), channel_id=1, source_target_pairs={{1,0},{2,1},{3,2},{4,3},{5,4},{6,5},{7,6},{8,7},{9,8},{10,9},{11,1... | collective-permute-start | bytes 61448 | tf_op jit(solution)/shard_map/ppermute | solution.py:45
  (42 other events, 105.1 us)
Sparse Core Ops, SparseCore 0:
  79.2 94.7 all-gather.5
  216.4 88.5 all-gather.7
  418.8 37.5 reduce-scatter.3

commit v4 on v2

--- a/solution.py
+++ b/solution.py
@@ -45,13 +45,32 @@
     return lax.ppermute(value, axis, [(source, source + steps) for source in range(initial, last)])
 
 
-def feature_map(columns):
-    key_size = columns.shape[1]
+def pair_pickers(key_size):
     upper_i, upper_j = np.triu_indices(key_size)
     factors = np.where(upper_i == upper_j, 1.0 / math.sqrt(2.0), 1.0).astype(np.float32)
-    products = columns[:, upper_i, :] * columns[:, upper_j, :] * jnp.asarray(factors)[None, :, None]
+    eye = np.eye(key_size, dtype=np.float32)
+    return (jnp.asarray(eye[upper_i]), jnp.asarray(eye[upper_j]), jnp.asarray(factors))
+
+
+def feature_map(columns):
+    pick_i, pick_j, factors = pair_pickers(columns.shape[1])
+    first = jnp.einsum("pk,hkl->hpl", pick_i, columns, precision=HIGHEST)
+    second = jnp.einsum("pk,hkl->hpl", pick_j, columns, precision=HIGHEST)
+    products = first * second * factors[None, :, None]
     constant = jnp.ones((columns.shape[0], 1, columns.shape[2]), jnp.float32)
-    return jnp.concatenate([constant, columns, products], axis=1)
+    return (jnp.concatenate([constant, columns, products], axis=1), (first, second))
+
+
+def feature_pull(parts, grad):
+    first, second = parts
+    key_size = KEY_DIM
+    pick_i, pick_j, factors = pair_pickers(key_size)
+    pair_grad = grad[:, 1 + key_size :] * factors[None, :, None]
+    return (
+        grad[:, 1 : 1 + key_size]
+        + jnp.einsum("pk,hpl->hkl", pick_i, pair_grad * second, precision=HIGHEST)
+        + jnp.einsum("pk,hpl->hkl", pick_j, pair_grad * first, precision=HIGHEST)
+    )
 
 
 def doc_place(doc_lengths, anchor, amount):
@@ -107,8 +126,8 @@
     key_cols = jnp.transpose(shaped[:, :, KEY_DIM : 2 * KEY_DIM], (1, 2, 0)) * scale_key
     values = shaped[:, :, 2 * KEY_DIM :]
     upstream = out_flat.reshape(length, local_heads, HEAD_DIM)
-    query_feat, query_pull = jax.vjp(feature_map, query_cols)
-    key_feat, key_pull = jax.vjp(feature_map, key_cols)
+    query_feat, query_parts = feature_map(query_cols)
+    key_feat, key_parts = feature_map(key_cols)
     feat_count = query_feat.shape[1]
     last_begin = begins[length - 1]
     has_start = (last_begin >= stretch_start).astype(jnp.float32).reshape(1)
@@ -197,8 +216,8 @@
     query_grad = jnp.transpose(grad_qblocks, (1, 2, 0, 3)).reshape(local_heads, feat_count, length)
     key_grad = jnp.transpose(grad_kblocks, (1, 2, 0, 3)).reshape(local_heads, feat_count, length)
     value_grad = grad_vblocks.reshape(length, local_heads, HEAD_DIM)
-    query_in = jnp.transpose(query_pull(query_grad)[0] * scale_key, (2, 0, 1))
-    key_in = jnp.transpose(key_pull(key_grad)[0] * scale_key, (2, 0, 1))
+    query_in = jnp.transpose(feature_pull(query_parts, query_grad) * scale_key, (2, 0, 1))
+    key_in = jnp.transpose(feature_pull(key_parts, key_grad) * scale_key, (2, 0, 1))
     return jnp.concatenate([query_in, key_in, value_grad], axis=2).reshape(
         length, local_heads * head_width
     )

time: 539 us -> 498 us (0.924)
  other arithmetic: 74.4 us -> 35.2 us
  matrix products: 58.9 us -> 69.8 us
  waiting for transfers between devices: 157 us -> 150 us
  local copies, waits for them, and re-layouts: 72 us -> 65.6 us
    scatter-add x4 -> x0, other arithmetic: 30.1 us -> none  [the longest x2 15.1 us: feature_map(): columns[:, upper_i, :] * columns[:, upper_j, :]]
    dot_general x0 -> x8, matrix products: none -> 13.3 us  [the longest x2 4.38 us: feature_pull(): jnp.einsum('pk,hpl->hkl', pick_j, pair_grad * first, precision=HIGHEST)]
    gather x4 -> x0, local copies, waits for them, and re-layouts: 10.9 us -> none  [the longest x2 6.1 us: feature_map(): columns[:, upper_j, :]]
    mul x2 -> x0, other arithmetic: 8.76 us -> none  [feature_map(): columns[:, upper_i, :] * columns[:, upper_j, :]]
    all_gather x2, waiting for transfers between devices: 99.2 us -> 93.7 us  [carried_in(): gathered = lax.all_gather(padded, axis).reshape(lax.axis_size(axis), -1)]
    unnamed x137 -> x147, local copies, waits for them, and re-layouts: 20.3 us -> 23.1 us
  transfers between devices with their start and end apart: 6 -> 6, of which waited for: 4 -> 4; matrix products, arithmetic and copies ran while one was open for 11% -> 13% of each run, Pallas kernels for 0% -> 0%
where the time goes in v4:
time: 498 us; the launch traced here: 489 us
  waiting for transfers between devices  150 us (30%)
  blocking collectives  136 us (27%)
  matrix products  69.8 us (14%)
  local copies, waits for them, and re-layouts  65.6 us (13%)
  other arithmetic  35.2 us (7%)
  between operations  16.1 us (3%)
  starting transfers between devices  15.7 us (3%)
    psum x1, blocking collectives, on_device(): grad_conv = lax.psum(weight_part, ('seq', 'head'))  95.7 us
    all_gather x2, waiting for transfers between devices, carried_in(): gathered = lax.all_gather(padded, axis).reshape(lax.axis_size(axis), -1)  93.7 us
    all_to_all x1, blocking collectives, on_device(): lax.all_to_all(grad_mixed, 'head', split_axis=0, concat_axis=1, tiled=True)  40.8 us
    all_to_all x1, waiting for transfers between devices, on_device(): lax.all_to_all(outgoing, 'head', split_axis=1, concat_axis=0, tiled=True)  32.1 us
    all_to_all x1, waiting for transfers between devices, on_device(): lax.all_to_all(out_grads, 'head', split_axis=1, concat_axis=0, tiled=True)  24.6 us
    unnamed x147, local copies, waits for them, and re-layouts  23.1 us
  transfers between devices with their start and end apart: 6, of which 4 were waited for; matrix products, arithmetic and copies ran while one was open for 13% of the time, Pallas kernels for 0%

profile of v4, /device:TPU:1, one launch (start us, length us, event | category | flops | bytes accessed | tf_op | source)
XLA Modules:
  0.0 489.3 jit_solution(8376621257306117411)
XLA Ops:
  8.1 4.0 collective-permute-start
  17.6 3.1 multiply_add_fusion
  20.7 5.9 %all-to-all-start = ((f32[128,8,320]{0,2,1:T(8,128)}), f32[128,8,320]{0,2,1:T(8,128)S(1)}, u32[]{:S(2)}, u32[]{:S(2)}) async-start(f32[128,8,320]{0,2,1:T(8,128)} %bitcast.244), calls=%async_computation | async-start | bytes 2621440 | tf_op jit(solution)/shard_map/all_to_all | solution.py:238
  29.3 32.1 %all-to-all-done = f32[128,8,320]{0,2,1:T(8,128)S(1)} async-done(((f32[128,8,320]{0,2,1:T(8,128)}), f32[128,8,320]{0,2,1:T(8,128)S(1)}, u32[]{:S(2)}, u32[]{:S(2)}) %all-to-all-start) | async-done | bytes 1310752 | tf_op jit(solution)/shard_map/all_to_all | solution.py:238
  73.0 3.3 multiply_reduce_fusion.3
  78.8 2.6 copy.226
  81.4 3.6 all-to-all-start.1
  89.5 24.6 %all-to-all-done.1 = f32[128,8,256]{0,2,1:T(8,128)S(1)} async-done(((f32[128,8,256]{0,2,1:T(8,128)}), f32[128,8,256]{0,2,1:T(8,128)S(1)}, u32[]{:S(2)}, u32[]{:S(2)}) %all-to-all-start.1) | async-done | bytes 1048608 | tf_op jit(solution)/shard_map/all_to_all | solution.py:239
  123.6 3.2 fusion.33
  126.9 5.2 %fusion.116 = (f32[8,2,128]{2,1,0:T(2,128)}, f32[8,2,128,128]{2,3,1,0:T(8,128)}) fusion(f32[2,153,8,128]{3,2,1,0:T(8,128)S(1)} %reshape.363, f32[2,153,8,128]{3,2,1,0:T(8,128)S(1)} %reshape.365, pred[8,128,128]{1,2,0:T(8,128)(4,1)S(1)} %copy-done.30), kind=kOutput, calls=%fused_computation.198 | convolution fusion | flops 481818624 | bytes 3694592 | tf_op jit(solution)/shard_map/bhft,bhfs->bhts/dot_general | solution.py:158
  132.0 38.4 %all-gather.3.cloned.1.call-done = f32[64,309,128]{2,1,0:T(8,128)} async-done(((f32[1,309,128]{2,1,0:T(8,128)}), f32[64,309,128]{2,1,0:T(8,128)}) %all-gather.3.cloned.1.call-update) | async-done | bytes 10125328 | tf_op jit(solution)/shard_map/all_gather | solution.py:35
  170.5 5.7 %copy.360 = f32[8,8,309,128]{3,1,2,0:T(8,128)S(1)} copy(f32[8,8,309,128]{3,2,1,0:T(8,128)} %bitcast.237) | data formatting | bytes 20250624
  181.5 3.3 convolution_add_fusion.1
  184.8 3.6 convolution_multiply_fusion.1
  191.5 2.5 copy.239
  205.8 2.7 fusion.37
  214.2 2.7 fusion.10
  222.9 2.6 reshape.374
  225.5 2.6 fusion.43
  228.1 2.8 fusion.50
  235.3 3.4 fusion.35
  238.7 3.4 convolution_bitcast_fusion.1
  242.1 3.4 fusion.36
  245.5 55.2 %all-gather.5.cloned.1.call-done = f32[64,309,128]{2,1,0:T(8,128)} async-done(((f32[1,309,128]{2,1,0:T(8,128)}), f32[64,309,128]{2,1,0:T(8,128)}) %all-gather.5.cloned.1.call-update) | async-done | bytes 10125328 | tf_op jit(solution)/shard_map/all_gather | solution.py:35
  300.7 5.9 %copy.359 = f32[8,8,309,128]{3,1,2,0:T(8,128)S(1)} copy(f32[8,8,309,128]{3,2,1,0:T(8,128)} %bitcast.238) | data formatting | bytes 20250624
  308.0 2.7 convolution_add_fusion
  310.8 4.6 convolution_multiply_fusion
  315.4 2.3 fusion.4
  326.1 3.5 fusion.8
  333.7 40.8 %all_to_all.51 = f32[8,128,320]{1,2,0:T(8,128)S(1)} all-to-all(f32[8,128,320]{1,2,0:T(8,128)S(1)} %copy.260), channel_id=1, replica_groups=mesh['seq'=64,'head'=8] {'head'}, dimensions={0} | all-to-all | bytes 2621440 | tf_op jit(solution)/shard_map/all_to_all | solution.py:243
  379.2 95.7 %psum.7 = f32[3,2560]{1,0:T(4,128)} all-reduce(f32[3,2560]{1,0:T(4,128)S(1)} %pad_maximum_fusion.5), channel_id=1, replica_groups=mesh['seq'=64,'head'=8] {'seq','head'}, use_global_device_ids=true, to_apply=%region_15.16 | all-reduce | flops 7680 | bytes 61440 | tf_op jit(solution)/shard_map/psum | solution.py:248
  476.4 4.2 fusion.15
  (249 shorter events, 93.5 us)
Async XLA Ops:
  8.1 9.0 %collective-permute-start = (f32[2,2560]{1,0:T(2,128)S(1)}, f32[2,2560]{1,0:T(2,128)S(1)}, u32[]{:S(2)}, u32[]{:S(2)}) collective-permute-start(f32[2,2560]{1,0:T(2,128)S(1)} %slice.122), channel_id=1, source_target_pairs={{0,1},{1,2},{2,3},{3,4},{4,5},{5,6},{6,7},{7,8},{8,9},{9,10},{10,1... | collective-permute-start | bytes 61448 | tf_op jit(solution)/shard_map/ppermute | solution.py:45
  17.1 3.6 copy-start.1
  20.7 40.7 %all-to-all-start = ((f32[128,8,320]{0,2,1:T(8,128)}), f32[128,8,320]{0,2,1:T(8,128)S(1)}, u32[]{:S(2)}, u32[]{:S(2)}) async-start(f32[128,8,320]{0,2,1:T(8,128)} %bitcast.244), calls=%async_computation | async-start | bytes 2621440 | tf_op jit(solution)/shard_map/all_to_all | solution.py:238
  26.6 143.8 %all-gather.3.cloned.1.call-start = ((), (), s32[]{:S(2)}) async-start(), calls=%async_computation.3 | async-start | bytes 10383360 | tf_op jit(solution)/shard_map/all_gather | solution.py:35
  28.0 45.0 %copy-start.56 = (f32[153]{0:T(256)}, f32[153]{0:T(256)S(1)}, u32[]{:S(2)}) copy-start(f32[153]{0:T(256)S(1)} %pad.23.clone) | copy-start | bytes 1840
  62.9 52.9 %copy-start = (f32[1024,2,160]{0,2,1:T(8,128)}, f32[1024,2,160]{0,2,1:T(8,128)S(1)}, u32[]{:S(2)}) copy-start(f32[1024,2,160]{0,2,1:T(8,128)S(1)} %reshape.362) | copy-start | bytes 3932164
  65.1 4.1 copy-start.5
  69.2 3.8 copy-start.20
  81.4 32.7 %all-to-all-start.1 = ((f32[128,8,256]{0,2,1:T(8,128)}), f32[128,8,256]{0,2,1:T(8,128)S(1)}, u32[]{:S(2)}, u32[]{:S(2)}) async-start(f32[128,8,256]{0,2,1:T(8,128)} %bitcast.10), calls=%async_computation.1 | async-start | bytes 2097152 | tf_op jit(solution)/shard_map/all_to_all | solution.py:239
  84.9 215.8 %all-gather.5.cloned.1.call-start = ((), (), s32[]{:S(2)}) async-start(), calls=%async_computation.4 | async-start | bytes 10383360 | tf_op jit(solution)/shard_map/all_gather | solution.py:35
  86.7 27.3 %copy-start.58 = (s32[8]{0:T(128)}, s32[8]{0:T(128)S(1)}, u32[]{:S(2)}) copy-start(s32[8]{0:T(128)S(1)} %get-tuple-element.19) | copy-start | bytes 100
  184.8 3.7 copy-start.16
  184.8 3.7 copy-start.14
  195.3 3.7 copy-start.48
  195.3 3.7 copy-start.51
  195.3 3.7 copy-start.26
  233.2 5.5 %copy-start.23 = (f32[8,2,128,128]{2,3,1,0:T(8,128)S(1)}, f32[8,2,128,128]{2,3,1,0:T(8,128)}, u32[]{:S(2)}) copy-start(f32[8,2,128,128]{2,3,1,0:T(8,128)} %copy-done.22) | copy-start | bytes 3145732
  300.7 5.9 %copy-start.69 = (pred[64]{0:T(512)(128)(4,1)S(1)}, pred[64]{0:T(512)(128)(4,1)}, u32[]{:S(2)}) copy-start(pred[64]{0:T(512)(128)(4,1)} %compare_and_fusion.1) | copy-start | bytes 196
  310.8 4.6 copy-start.18
  322.4 3.8 copy-start.13
  322.4 3.8 copy-start.15
  322.4 3.8 copy-start.34
  333.4 41.1 %copy-start.61 = (f32[128]{0:T(128)S(1)}, f32[128]{0:T(128)}, u32[]{:S(2)}) copy-start(f32[128]{0:T(128)} %copy-done.60) | copy-start | bytes 1540
  333.4 41.1 %copy-start.63 = (f32[128]{0:T(128)S(1)}, f32[128]{0:T(128)}, u32[]{:S(2)}) copy-start(f32[128]{0:T(128)} %copy-done.62) | copy-start | bytes 1540
  333.7 40.8 %copy-start.2 = (f32[128,2560]{0,1:T(8,128)S(1)}, f32[128,2560]{0,1:T(8,128)}, u32[]{:S(2)}) copy-start(f32[128,2560]{0,1:T(8,128)} %copy-done.1) | copy-start | bytes 3932164
  333.7 40.8 %copy-start.4 = (f32[2,2560]{0,1:T(8,128)S(1)}, f32[2,2560]{0,1:T(8,128)}, u32[]{:S(2)}) copy-start(f32[2,2560]{0,1:T(8,128)} %copy-done.3) | copy-start | bytes 61444
  376.7 99.6 %copy-start.41 = (f32[2560]{0:T(1024)S(1)}, f32[2560]{0:T(1024)}, u32[]{:S(2)}) copy-start(f32[2560]{0:T(1024)} %copy-done.40) | copy-start | bytes 30724
  376.8 99.6 %copy-start.43 = (f32[2560]{0:T(1024)S(1)}, f32[2560]{0:T(1024)}, u32[]{:S(2)}) copy-start(f32[2560]{0:T(1024)} %copy-done.42) | copy-start | bytes 30724
  376.8 99.6 %copy-start.45 = (f32[2560]{0:T(1024)S(1)}, f32[2560]{0:T(1024)}, u32[]{:S(2)}) copy-start(f32[2560]{0:T(1024)} %copy-done.44) | copy-start | bytes 30724
  376.8 99.6 %copy-start.65 = (f32[128]{0:T(128)S(1)}, f32[128]{0:T(128)}, u32[]{:S(2)}) copy-start(f32[128]{0:T(128)} %get-tuple-element.32) | copy-start | bytes 1540
  376.8 99.6 %copy-start.66 = (f32[128]{0:T(128)S(1)}, f32[128]{0:T(128)}, u32[]{:S(2)}) copy-start(f32[128]{0:T(128)} %get-tuple-element.34) | copy-start | bytes 1540
  377.2 97.6 %collective-permute-start.1 = (f32[2,2560]{1,0:T(2,128)S(1)}, f32[2,2560]{1,0:T(2,128)S(1)}, u32[]{:S(2)}, u32[]{:S(2)}) collective-permute-start(f32[2,2560]{1,0:T(2,128)S(1)} %copy.261), channel_id=1, source_target_pairs={{1,0},{2,1},{3,2},{4,3},{5,4},{6,5},{7,6},{8,7},{9,8},{10,9},{11,1... | collective-permute-start | bytes 61448 | tf_op jit(solution)/shard_map/ppermute | solution.py:45
  (45 other events, 95.8 us)
Sparse Core Ops, SparseCore 0:
  78.9 91.5 all-gather.2
  212.2 88.5 all-gather.4

commit v5 on v4

--- a/solution.py
+++ b/solution.py
@@ -11,6 +11,7 @@
 
 
 HIGHEST = lax.Precision.HIGHEST
+FAST = lax.Precision.HIGH
 
 
 def segment_sum(gathered, flags, here, reverse):
@@ -133,7 +134,7 @@
     has_start = (last_begin >= stretch_start).astype(jnp.float32).reshape(1)
     tail_mask = (begins == last_begin).astype(jnp.float32)
     tail_feat = key_feat * tail_mask[None, None, :]
-    tail_state = jnp.einsum("hfl,lhe->hfe", tail_feat, values, precision=HIGHEST)
+    tail_state = jnp.einsum("hfl,lhe->hfe", tail_feat, values, precision=FAST)
     tail_norm = jnp.sum(tail_feat, axis=2)
     prefix = carried_in(tail_state, tail_norm, has_start, None, "seq", False)
     flags = prefix[2]
@@ -155,10 +156,10 @@
     behind_w = ((order[None, :] > order[:, None]) & (before[None, :] == upto[:, None])).astype(jnp.float32)
     behind_p = (upto[blocks - 1] == upto).astype(jnp.float32)
     scores = jnp.where(
-        allowed[:, None], jnp.einsum("bhft,bhfs->bhts", query_blk, key_blk, precision=HIGHEST), 0.0
+        allowed[:, None], jnp.einsum("bhft,bhfs->bhts", query_blk, key_blk, precision=FAST), 0.0
     )
     tail_keys = key_blk * block_tail[:, None, None, :]
-    tail_states = jnp.einsum("bhfs,bshe->bhfe", tail_keys, value_blk, precision=HIGHEST)
+    tail_states = jnp.einsum("bhfs,bshe->bhfe", tail_keys, value_blk, precision=FAST)
     tail_norms = jnp.sum(tail_keys, axis=3)
     carry_state = jnp.einsum("bc,chfe->bhfe", ahead_w, tail_states, precision=HIGHEST) + ahead_p[
         :, None, None, None
@@ -166,11 +167,11 @@
     carry_norm = jnp.einsum("bc,chf->bhf", ahead_w, tail_norms, precision=HIGHEST) + ahead_p[
         :, None, None
     ] * prefix[1][None]
-    numerators = jnp.einsum("bhts,bshe->bthe", scores, value_blk, precision=HIGHEST) + from_carry[
+    numerators = jnp.einsum("bhts,bshe->bthe", scores, value_blk, precision=FAST) + from_carry[
         :, :, None, None
-    ] * jnp.einsum("bhft,bhfe->bthe", query_blk, carry_state, precision=HIGHEST)
+    ] * jnp.einsum("bhft,bhfe->bthe", query_blk, carry_state, precision=FAST)
     denominators = jnp.sum(scores, axis=3) + from_carry[:, None, :] * jnp.einsum(
-        "bhft,bhf->bht", query_blk, carry_norm, precision=HIGHEST
+        "bhft,bhf->bht", query_blk, carry_norm, precision=FAST
     )
     denom_rows = jnp.transpose(denominators, (0, 2, 1)).reshape(length, local_heads)
     attended = numerators.reshape(length, local_heads, HEAD_DIM) / denom_rows[:, :, None]
@@ -178,41 +179,41 @@
     scalar_grad = -jnp.sum(upstream * attended, axis=2) / denom_rows
     lead_mask = (begins < stretch_start).astype(jnp.float32)
     lead_feat = query_feat * lead_mask[None, None, :]
-    lead_state = jnp.einsum("hfl,lhe->hfe", lead_feat, grad_num, precision=HIGHEST)
-    lead_norm = jnp.einsum("hfl,lh->hf", lead_feat, scalar_grad, precision=HIGHEST)
+    lead_state = jnp.einsum("hfl,lhe->hfe", lead_feat, grad_num, precision=FAST)
+    lead_norm = jnp.einsum("hfl,lh->hf", lead_feat, scalar_grad, precision=FAST)
     suffix = carried_in(lead_state, lead_norm, jnp.zeros((0,), jnp.float32), flags, "seq", True)
     grad_blk = grad_num.reshape(blocks, block_len, local_heads, HEAD_DIM)
     scalar_cols = jnp.transpose(scalar_grad.reshape(blocks, block_len, local_heads), (0, 2, 1))
     dscores = jnp.where(
         allowed[:, None],
-        jnp.einsum("bthe,bshe->bhts", grad_blk, value_blk, precision=HIGHEST)
+        jnp.einsum("bthe,bshe->bhts", grad_blk, value_blk, precision=FAST)
         + scalar_cols[:, :, :, None],
         0.0,
     )
     lead_blk = query_blk * from_carry[:, None, None, :]
-    lead_states = jnp.einsum("bhft,bthe->bhfe", lead_blk, grad_blk, precision=HIGHEST)
-    lead_norms = jnp.einsum("bhft,bht->bhf", lead_blk, scalar_cols, precision=HIGHEST)
+    lead_states = jnp.einsum("bhft,bthe->bhfe", lead_blk, grad_blk, precision=FAST)
+    lead_norms = jnp.einsum("bhft,bht->bhf", lead_blk, scalar_cols, precision=FAST)
     back_state = jnp.einsum("bc,chfe->bhfe", behind_w, lead_states, precision=HIGHEST) + behind_p[
         :, None, None, None
     ] * suffix[0][None]
     back_norm = jnp.einsum("bc,chf->bhf", behind_w, lead_norms, precision=HIGHEST) + behind_p[
         :, None, None
     ] * suffix[1][None]
-    grad_qblocks = jnp.einsum("bhts,bhfs->bhft", dscores, key_blk, precision=HIGHEST) + from_carry[
+    grad_qblocks = jnp.einsum("bhts,bhfs->bhft", dscores, key_blk, precision=FAST) + from_carry[
         :, None, None, :
     ] * (
-        jnp.einsum("bhfe,bthe->bhft", carry_state, grad_blk, precision=HIGHEST)
+        jnp.einsum("bhfe,bthe->bhft", carry_state, grad_blk, precision=FAST)
         + carry_norm[:, :, :, None] * scalar_cols[:, :, None, :]
     )
-    grad_kblocks = jnp.einsum("bhts,bhft->bhfs", dscores, query_blk, precision=HIGHEST) + block_tail[
+    grad_kblocks = jnp.einsum("bhts,bhft->bhfs", dscores, query_blk, precision=FAST) + block_tail[
         :, None, None, :
     ] * (
-        jnp.einsum("bhfe,bshe->bhfs", back_state, value_blk, precision=HIGHEST)
+        jnp.einsum("bhfe,bshe->bhfs", back_state, value_blk, precision=FAST)
         + back_norm[:, :, :, None]
     )
-    grad_vblocks = jnp.einsum("bhts,bthe->bshe", scores, grad_blk, precision=HIGHEST) + block_tail[
+    grad_vblocks = jnp.einsum("bhts,bthe->bshe", scores, grad_blk, precision=FAST) + block_tail[
         :, :, None, None
-    ] * jnp.einsum("bhfs,bhfe->bshe", key_blk, back_state, precision=HIGHEST)
+    ] * jnp.einsum("bhfs,bhfe->bshe", key_blk, back_state, precision=FAST)
     query_grad = jnp.transpose(grad_qblocks, (1, 2, 0, 3)).reshape(local_heads, feat_count, length)
     key_grad = jnp.transpose(grad_kblocks, (1, 2, 0, 3)).reshape(local_heads, feat_count, length)
     value_grad = grad_vblocks.reshape(length, local_heads, HEAD_DIM)
@@ -234,10 +235,13 @@
     token_begins, token_offsets = doc_place(doc_lengths, token_base, row_count + 2)
     leading = passed_along(projected[row_count - 2 :], ("seq", "head"), 1)
     outgoing = conv_forward(projected, leading, conv_weight, token_offsets)
-    arrived, upstream = (
-        lax.all_to_all(outgoing, "head", split_axis=1, concat_axis=0, tiled=True),
-        lax.all_to_all(out_grads, "head", split_axis=1, concat_axis=0, tiled=True),
-    )
+    mixed_width = outgoing.shape[1] // head_count
+    both = jnp.concatenate(
+        [outgoing.reshape(row_count, head_count, -1), out_grads.reshape(row_count, head_count, -1)],
+        axis=2,
+    ).reshape(row_count, -1)
+    landed = lax.all_to_all(both, "head", split_axis=1, concat_axis=0, tiled=True)
+    arrived, upstream = (landed[:, :mixed_width], landed[:, mixed_width:])
     group_begins, group_offsets = doc_place(doc_lengths, stretch_start, group_len + 2)
     grad_mixed = attention_grads(arrived, upstream, group_begins[:group_len], stretch_start)
     returned = lax.all_to_all(grad_mixed, "head", split_axis=0, concat_axis=1, tiled=True)

time: 498 us -> 512 us (1.028)
  waiting for transfers between devices: 150 us -> 181 us
  matrix products: 69.8 us -> 53.5 us
    all_gather x2, waiting for transfers between devices: 93.7 us -> 126 us  [carried_in(): gathered = lax.all_gather(padded, axis).reshape(lax.axis_size(axis), -1)]
    dot_general x17, matrix products: 48.7 us -> 32.7 us  [the longest x1 3.6 us: attention_grads(): jnp.einsum('bhft,bhfs->bhts', query_blk, key_blk, precision=FAST)]
    all_to_all x2 -> x1, waiting for transfers between devices: 56.7 us -> 54.6 us  [on_device(): lax.all_to_all(both, 'head', split_axis=1, concat_axis=0, tiled=True)]
    unnamed x147 -> x152, local copies, waits for them, and re-layouts: 23.1 us -> 25 us
  transfers between devices with their start and end apart: 6 -> 5, of which waited for: 4 -> 3; matrix products, arithmetic and copies ran while one was open for 13% -> 12% of each run, Pallas kernels for 0% -> 0%
where the time goes in v5:
time: 512 us; the launch traced here: 505 us
  waiting for transfers between devices  181 us (35%)
  blocking collectives  136 us (27%)
  local copies, waits for them, and re-layouts  68.7 us (13%)
  matrix products  53.5 us (10%)
  other arithmetic  37.2 us (7%)
  between operations  15.9 us (3%)
  starting transfers between devices  12.1 us (2%)
    all_gather x2, waiting for transfers between devices, carried_in(): gathered = lax.all_gather(padded, axis).reshape(lax.axis_size(axis), -1)  126 us
    psum x1, blocking collectives, on_device(): grad_conv = lax.psum(weight_part, ('seq', 'head'))  95.7 us
    all_to_all x1, waiting for transfers between devices, on_device(): lax.all_to_all(both, 'head', split_axis=1, concat_axis=0, tiled=True)  54.6 us
    all_to_all x1, blocking collectives, on_device(): lax.all_to_all(grad_mixed, 'head', split_axis=0, concat_axis=1, tiled=True)  40.8 us
    unnamed x152, local copies, waits for them, and re-layouts  25 us
  transfers between devices with their start and end apart: 5, of which 3 were waited for; matrix products, arithmetic and copies ran while one was open for 12% of the time, Pallas kernels for 0%

profile of v5, /device:TPU:1, one launch (start us, length us, event | category | flops | bytes accessed | tf_op | source)
XLA Modules:
  0.0 504.9 jit_solution(17890270033826889849)
XLA Ops:
  8.1 4.0 collective-permute-start
  19.2 2.4 multiply_add_fusion
  23.2 5.9 %all-to-all-start = ((f32[128,8,576]{0,2,1:T(8,128)}), f32[128,8,576]{0,2,1:T(8,128)S(1)}, u32[]{:S(2)}, u32[]{:S(2)}) async-start(f32[128,8,576]{0,2,1:T(8,128)} %pad_maximum_fusion), calls=%async_computation | async-start | bytes 4718592 | tf_op jit(solution)/shard_map/all_to_all | solution.py:243
  31.8 54.6 %all-to-all-done = f32[128,8,576]{0,2,1:T(8,128)S(1)} async-done(((f32[128,8,576]{0,2,1:T(8,128)}), f32[128,8,576]{0,2,1:T(8,128)S(1)}, u32[]{:S(2)}, u32[]{:S(2)}) %all-to-all-start) | async-done | bytes 2359328 | tf_op jit(solution)/shard_map/all_to_all | solution.py:243
  92.2 2.3 multiply_multiply_fusion
  97.6 3.3 multiply_reduce_fusion.3
  114.2 2.8 fusion.116
  119.0 3.6 fusion.117
  122.6 72.5 %all-gather.3.cloned.1.call-done = f32[64,309,128]{2,1,0:T(8,128)} async-done(((f32[1,309,128]{2,1,0:T(8,128)}), f32[64,309,128]{2,1,0:T(8,128)}) %all-gather.3.cloned.1.call-update) | async-done | bytes 10125328 | tf_op jit(solution)/shard_map/all_gather | solution.py:36
  195.1 5.7 %copy.358 = f32[8,8,309,128]{3,1,2,0:T(8,128)S(1)} copy(f32[8,8,309,128]{3,2,1,0:T(8,128)} %bitcast.255) | data formatting | bytes 20250624
  206.3 2.9 convolution_add_fusion.1
  209.2 2.0 convolution_multiply_fusion.1
  213.6 2.6 copy.238
  220.6 2.1 multiply_reduce_fusion.4
  226.6 2.0 fusion.37
  234.8 2.6 copy.230
  239.5 2.5 fusion.10
  247.7 2.5 reshape.379
  250.3 2.6 fusion.43
  253.0 2.8 fusion.50
  255.7 2.2 copy.256
  259.9 2.4 fusion.35
  262.3 2.7 convolution_bitcast_fusion.1
  267.0 53.9 %all-gather.5.cloned.1.call-done = f32[64,309,128]{2,1,0:T(8,128)} async-done(((f32[1,309,128]{2,1,0:T(8,128)}), f32[64,309,128]{2,1,0:T(8,128)}) %all-gather.5.cloned.1.call-update) | async-done | bytes 10125328 | tf_op jit(solution)/shard_map/all_gather | solution.py:36
  320.9 5.7 %copy.357 = f32[8,8,309,128]{3,1,2,0:T(8,128)S(1)} copy(f32[8,8,309,128]{3,2,1,0:T(8,128)} %bitcast.254) | data formatting | bytes 20250624
  328.0 2.8 convolution_add_fusion
  330.8 3.0 convolution_multiply_fusion
  341.3 2.2 copy.257
  349.5 40.8 %all_to_all.35 = f32[8,128,320]{1,2,0:T(8,128)S(1)} all-to-all(f32[8,128,320]{1,2,0:T(8,128)S(1)} %copy.259), channel_id=1, replica_groups=mesh['seq'=64,'head'=8] {'head'}, dimensions={0} | all-to-all | bytes 2621440 | tf_op jit(solution)/shard_map/all_to_all | solution.py:247
  390.3 2.2 multiply_reduce_fusion.1
  394.9 95.7 %psum.7 = f32[3,2560]{1,0:T(4,128)} all-reduce(f32[3,2560]{1,0:T(4,128)S(1)} %pad_maximum_fusion.6), channel_id=1, replica_groups=mesh['seq'=64,'head'=8] {'seq','head'}, use_global_device_ids=true, to_apply=%region_15.16 | all-reduce | flops 7680 | bytes 61440 | tf_op jit(solution)/shard_map/psum | solution.py:252
  492.2 4.2 fusion.15
  (253 shorter events, 89.4 us)
Async XLA Ops:
  8.1 10.6 %collective-permute-start = (f32[2,2560]{1,0:T(2,128)S(1)}, f32[2,2560]{1,0:T(2,128)S(1)}, u32[]{:S(2)}, u32[]{:S(2)}) collective-permute-start(f32[2,2560]{1,0:T(2,128)S(1)} %slice.128), channel_id=1, source_target_pairs={{0,1},{1,2},{2,3},{3,4},{4,5},{5,6},{6,7},{7,8},{8,9},{9,10},{10,1... | collective-permute-start | bytes 61448 | tf_op jit(solution)/shard_map/ppermute | solution.py:46
  14.4 4.7 copy-start.62
  14.4 4.7 copy-start.64
  15.4 3.7 copy-start.45
  15.4 3.7 copy-start.47
  15.4 3.7 copy-start.49
  23.2 63.2 %all-to-all-start = ((f32[128,8,576]{0,2,1:T(8,128)}), f32[128,8,576]{0,2,1:T(8,128)S(1)}, u32[]{:S(2)}, u32[]{:S(2)}) async-start(f32[128,8,576]{0,2,1:T(8,128)} %pad_maximum_fusion), calls=%async_computation | async-start | bytes 4718592 | tf_op jit(solution)/shard_map/all_to_all | solution.py:243
  29.1 166.0 %all-gather.3.cloned.1.call-start = ((), (), s32[]{:S(2)}) async-start(), calls=%async_computation.2 | async-start | bytes 10383360 | tf_op jit(solution)/shard_map/all_gather | solution.py:36
  30.5 67.1 %copy-start.58 = (f32[153]{0:T(256)}, f32[153]{0:T(256)S(1)}, u32[]{:S(2)}) copy-start(f32[153]{0:T(256)S(1)} %pad.23.clone) | copy-start | bytes 1840
  90.3 4.1 copy-start.10
  91.1 3.4 copy-start.28
  94.5 3.1 copy-start.22
  103.4 5.4 %copy-start.21 = (f32[2,153,1024]{2,1,0:T(8,128)S(1)}, f32[2,153,1024]{2,1,0:T(8,128)}, u32[]{:S(2)}) copy-start(f32[2,153,1024]{2,1,0:T(8,128)} %get-tuple-element.29) | copy-start | bytes 3760132
  103.4 217.5 %all-gather.5.cloned.1.call-start = ((), (), s32[]{:S(2)}) async-start(), calls=%async_computation.3 | async-start | bytes 10383360 | tf_op jit(solution)/shard_map/all_gather | solution.py:36
  104.9 4.0 copy-start.60
  217.4 3.2 copy-start.42
  217.4 3.2 copy-start.53
  217.4 3.2 copy-start.26
  258.0 4.3 copy-start.17
  320.9 5.7 %copy-start.71 = (pred[64]{0:T(512)(128)(4,1)S(1)}, pred[64]{0:T(512)(128)(4,1)}, u32[]{:S(2)}) copy-start(pred[64]{0:T(512)(128)(4,1)} %compare_and_fusion.1) | copy-start | bytes 196
  339.7 3.8 copy-start.2
  339.7 3.8 copy-start.19
  349.2 41.1 %copy-start.63 = (f32[128]{0:T(128)S(1)}, f32[128]{0:T(128)}, u32[]{:S(2)}) copy-start(f32[128]{0:T(128)} %copy-done.62) | copy-start | bytes 1540
  349.2 41.1 %copy-start.65 = (f32[128]{0:T(128)S(1)}, f32[128]{0:T(128)}, u32[]{:S(2)}) copy-start(f32[128]{0:T(128)} %copy-done.64) | copy-start | bytes 1540
  349.5 40.8 %copy-start.7 = (f32[128,2560]{0,1:T(8,128)S(1)}, f32[128,2560]{0,1:T(8,128)}, u32[]{:S(2)}) copy-start(f32[128,2560]{0,1:T(8,128)} %copy-done.6) | copy-start | bytes 3932164
  349.5 40.8 %copy-start.9 = (f32[2,2560]{0,1:T(8,128)S(1)}, f32[2,2560]{0,1:T(8,128)}, u32[]{:S(2)}) copy-start(f32[2,2560]{0,1:T(8,128)} %copy-done.8) | copy-start | bytes 61444
  392.5 99.6 %copy-start.46 = (f32[2560]{0:T(1024)S(1)}, f32[2560]{0:T(1024)}, u32[]{:S(2)}) copy-start(f32[2560]{0:T(1024)} %copy-done.45) | copy-start | bytes 30724
  392.5 99.6 %copy-start.48 = (f32[2560]{0:T(1024)S(1)}, f32[2560]{0:T(1024)}, u32[]{:S(2)}) copy-start(f32[2560]{0:T(1024)} %copy-done.47) | copy-start | bytes 30724
  392.6 99.6 %copy-start.50 = (f32[2560]{0:T(1024)S(1)}, f32[2560]{0:T(1024)}, u32[]{:S(2)}) copy-start(f32[2560]{0:T(1024)} %copy-done.49) | copy-start | bytes 30724
  392.6 99.6 %copy-start.67 = (f32[128]{0:T(128)S(1)}, f32[128]{0:T(128)}, u32[]{:S(2)}) copy-start(f32[128]{0:T(128)} %get-tuple-element.34) | copy-start | bytes 1540
  392.6 99.6 %copy-start.68 = (f32[128]{0:T(128)S(1)}, f32[128]{0:T(128)}, u32[]{:S(2)}) copy-start(f32[128]{0:T(128)} %get-tuple-element.36) | copy-start | bytes 1540
  393.0 97.7 %collective-permute-start.1 = (f32[2,2560]{1,0:T(2,128)S(1)}, f32[2,2560]{1,0:T(2,128)S(1)}, u32[]{:S(2)}, u32[]{:S(2)}) collective-permute-start(f32[2,2560]{1,0:T(2,128)S(1)} %copy.260), channel_id=1, source_target_pairs={{1,0},{2,1},{3,2},{4,3},{5,4},{6,5},{7,6},{8,7},{9,8},{10,9},{11,1... | collective-permute-start | bytes 61448 | tf_op jit(solution)/shard_map/ppermute | solution.py:46
  (45 other events, 89.8 us)
Sparse Core Ops, SparseCore 0:
  103.5 91.5 all-gather.2
  232.4 88.5 all-gather.4
